TPU v7x, 256 devices: a whole 4x4x8 slice. The times are simulated.
256 devices in a mesh: blk: 32 (over y_hi, z, core), col: 8 (over y_lo, x).
Axes of the slice: x: 4, y: 4 (y_hi: 2, y_lo: 2; y = y_hi * 2 + y_lo), z: 8, core: 2. Of those that a mesh axis runs over, the one named last changes fastest.
Arguments:
- a_blocks: float32 [32, 128, 384, 128], P('col', None, 'blk'), may hold values from -6 to 6
- a_mask: int32 [32, 384], P('col', 'blk'), may hold values 0 or 1
- b_blocks: float32 [384, 128, 32, 128], P('blk', None, 'col'), may hold values from -0.0546875 to 0.0546875
- b_mask: int32 [384, 32], P('blk', 'col'), may hold values 0 or 1
- c_mask: int32 [32, 32], P('blk', 'col'), may hold values 0 or 1
Outputs:
- product: float32 [32, 128, 32, 128], P('blk', None, 'col')
All inputs are finite; a program needn't handle non-finite values. No bound on the sum of `a_mask` or of `b_mask` or of `c_mask` on one device may be relied on, other than what follows from the above.
Results may differ from a plain program's by a relative error of at most 0.000071.
Values sent between devices are 32-bit elements; how exact they have to be, the bound alone decides.
No kernel may reach another device: no remote copies, remote signals or barrier semaphores. Data moves between devices by JAX's collectives and lax.ppermute only.
A program may use at most 128 MiB of HBM per device.

v0:
```python
import jax
import jax.numpy as jnp
from jax import lax
from jax.sharding import PartitionSpec as P


def shards(a_blocks, a_mask, b_blocks, b_mask, c_mask):
    masked_a = a_blocks * a_mask.astype(jnp.float32)[:, None, :, None]
    masked_b = b_blocks * b_mask.astype(jnp.float32)[:, None, :, None]
    col_count = masked_b.shape[2]
    block_side = masked_b.shape[3]
    flat_b = masked_b.reshape(masked_b.shape[0] * masked_b.shape[1], col_count * block_side)
    piece = lax.all_gather(masked_a, "col", axis=0, tiled=True)
    count = piece.shape[0]
    flat_piece = piece.reshape(count * piece.shape[1], piece.shape[2] * piece.shape[3])
    result = jnp.dot(
        flat_piece, flat_b, precision=lax.Precision.HIGHEST, preferred_element_type=jnp.float32
    )
    partial_value = result.reshape(count, piece.shape[1], col_count, block_side)
    owned = lax.psum_scatter(partial_value, "blk", scatter_dimension=0, tiled=True)
    return owned * c_mask.astype(jnp.float32)[:, None, :, None]


def solution(mesh):
    return jax.shard_map(
        shards,
        mesh=mesh,
        in_specs=(
            P("col", None, "blk", None),
            P("col", "blk"),
            P("blk", None, "col", None),
            P("blk", "col"),
            P("blk", "col"),
        ),
        out_specs=P("blk", None, "col", None),
        check_vma=False,
    )
```

profile of v0, /device:TPU:24, one launch (start us, length us, event | category | flops | bytes accessed | tf_op | source)
XLA Modules:
  0.0 533.7 jit_solution(895382643046142250)
XLA Ops:
  6.5 0.0 all-gather.2.cloned.1.call-start
  6.5 0.7 convert_element_type.9
  7.2 3.9 broadcast_multiply_fusion.1
  11.1 0.0 copy-start.2
  11.1 0.0 copy-start
  11.1 0.0 all-gather.2.cloned.1.call-update
  11.1 0.0 reduce-scatter.2.cloned.1.call-start
  11.2 0.6 copy-done.2
  11.8 0.1 copy.16
  11.9 1.1 copy-done
  13.0 0.7 broadcast_multiply_fusion
  13.7 0.3 copy.25
  14.1 2.3 copy.17
  16.4 0.0 copy-start.1
  16.4 248.6 %all-gather.2.cloned.1.call-done = f32[32,128,12,128]{3,1,2,0:T(8,128)} async-done(((f32[4,128,12,128]{3,1,2,0:T(8,128)}), f32[32,128,12,128]{3,1,2,0:T(8,128)}) %all-gather.2.cloned.1.call-update) | async-done | bytes 25165840 | tf_op jit(solution)/shard_map/all_gather | solution.py:13
  265.0 24.6 %copy.15 = f32[32,128,12,128]{1,3,2,0:T(8,128)} copy(f32[32,128,12,128]{3,1,2,0:T(8,128)} %all-gather.2.cloned.1.call-done) | data formatting | bytes 50331648 | tf_op jit(solution)/shard_map/all_gather | solution.py:13
  289.7 0.0 copy-done.1
  289.7 82.6 %fusion = f32[32,128,4,128]{3,1,2,0:T(8,128)} fusion(f32[32,128,1536,1]{1,2,3,0:T(8,128)} %bitcast.20, f32[4,128,1536,1]{2,1,0,3:T(8,128)S(1)} %bitcast.23), kind=kOutput, calls=%fused_computation.5 | convolution fusion | flops 38654705664 | bytes 36700160 | tf_op jit(solution)/shard_map/dot_general | solution.py:16
  372.2 0.0 copy-start.3
  372.3 0.0 reduce-scatter.2.cloned.1.call-update
  372.3 0.6 copy-done.3
  372.9 152.1 %reduce-scatter.2.cloned.1.call-done = f32[1,128,4,128]{3,1,2,0:T(8,128)} async-done(((f32[32,128,4,128]{3,1,2,0:T(8,128)}), f32[1,128,4,128]{3,1,2,0:T(8,128)}) %reduce-scatter.2.cloned.1.call-update) | async-done | bytes 262160 | tf_op jit(solution)/shard_map/reduce_scatter | solution.py:20
  525.0 1.0 broadcast_multiply_fusion.2
  526.0 0.9 copy.19
  (2 shorter events, 0.0 us)
Async XLA Ops:
  6.5 258.5 %all-gather.2.cloned.1.call-start = ((), (), s32[]{:S(2)}) async-start(), calls=%async_computation.1 | async-start | bytes 28311552 | tf_op jit(solution)/shard_map/all_gather | solution.py:13
  11.1 0.7 copy-start.2
  11.1 1.9 copy-start
  11.1 513.8 %reduce-scatter.2.cloned.1.call-start = ((), (), s32[]{:S(2)}) async-start(), calls=%async_computation.2 | async-start | bytes 8650752 | tf_op jit(solution)/shard_map/reduce_scatter | solution.py:20
  16.4 273.3 %copy-start.1 = (f32[512,1536]{1,0:T(8,128)S(1)}, f32[512,1536]{1,0:T(8,128)}, u32[]{:S(2)}) copy-start(f32[512,1536]{1,0:T(8,128)} %copy.17) | copy-start | bytes 9437188
  372.2 0.7 copy-start.3
Sparse Core Ops, SparseCore 0:
  11.3 253.7 all-gather.1
  372.4 152.5 reduce-scatter.1
where the time goes:
time: 536 us; the launch traced here: 534 us
  waiting for transfers between devices  401 us (75%)
  matrix products  82.6 us (15%)
  local copies, waits for them, and re-layouts  30.6 us (6%)
  between operations  13.4 us (2%)
  other arithmetic  6.34 us (1%)
    all_gather x1, waiting for transfers between devices, shards(): piece = lax.all_gather(masked_a, 'col', axis=0, tiled=True)  249 us
    reduce_scatter x1, waiting for transfers between devices, shards(): lax.psum_scatter(partial_value, 'blk', scatter_dimension=0, tiled=True)  152 us
    dot_general x1, matrix products, shards(): jnp.dot(flat_piece, flat_b, precision=lax.Precision.HIGHEST, preferred_el...  82.6 us
    all_gather x1, local copies, waits for them, and re-layouts, shards(): piece = lax.all_gather(masked_a, 'col', axis=0, tiled=True)  24.6 us
  transfers between devices with their start and end apart: 2, of which 2 were waited for; matrix products, arithmetic and copies ran while one was open for 1% of the time, Pallas kernels for 0%

commit v1 on v0

v1 whole, which is shorter than its diff:
```python
import jax
import jax.numpy as jnp
from jax import lax
from jax.sharding import Mesh
from jax.sharding import PartitionSpec as P

CHUNKS = 2


def owner_perm(blk, ylo, xs):
    half = blk // 2
    pairs = []
    for i in range(blk):
        hr, t = divmod(i, half)
        for y in range(ylo):
            for x in range(xs):
                src = (i * ylo + y) * xs + x
                dst = ((half * y + t) * ylo + (y ^ hr)) * xs + x
                pairs.append((src, dst))
    return pairs


def shards(a_blocks, a_mask, b_blocks, b_mask, c_mask, *, perm):
    masked_a = a_blocks * a_mask.astype(jnp.float32)[:, None, :, None]
    masked_b = b_blocks * b_mask.astype(jnp.float32)[:, None, :, None]
    rows_a = lax.all_gather(masked_a, "x", axis=0, tiled=True)
    other_b = lax.ppermute(masked_b, "ylo", [(0, 1), (1, 0)])
    rows = rows_a.shape[0] * rows_a.shape[1]
    depth = rows_a.shape[2] * rows_a.shape[3]
    flat_a = rows_a.reshape(rows, depth)
    side = masked_b.shape[3]
    width = masked_b.shape[2] * side
    own_flat = masked_b.reshape(depth, width)
    other_flat = other_b.reshape(depth, width)
    step = width // CHUNKS
    pieces = []
    for c in range(CHUNKS):
        parts = []
        for src in (own_flat, other_flat):
            part = jnp.dot(
                flat_a,
                src[:, c * step:(c + 1) * step],
                precision=lax.Precision.HIGHEST,
                preferred_element_type=jnp.float32,
            )
            parts.append(part.reshape(rows_a.shape[0], rows_a.shape[1], step // side, side))
        stacked = jnp.concatenate(parts, axis=0)
        pieces.append(lax.psum_scatter(stacked, "blk", scatter_dimension=0, tiled=True))
    owned = jnp.concatenate(pieces, axis=2)
    owned = lax.ppermute(owned, ("blk", "ylo", "x"), perm)
    return owned * c_mask.astype(jnp.float32)[:, None, :, None]


def solution(mesh):
    blk = mesh.shape["blk"]
    col = mesh.shape["col"]
    xs = 4
    ylo = col // xs
    sub = Mesh(mesh.devices.reshape(blk, ylo, xs), ("blk", "ylo", "x"))
    perm = owner_perm(blk, ylo, xs)
    cols = ("ylo", "x")

    def body(a_blocks, a_mask, b_blocks, b_mask, c_mask):
        return shards(a_blocks, a_mask, b_blocks, b_mask, c_mask, perm=perm)

    return jax.shard_map(
        body,
        mesh=sub,
        in_specs=(
            P(cols, None, "blk", None),
            P(cols, "blk"),
            P("blk", None, cols, None),
            P("blk", cols),
            P("blk", cols),
        ),
        out_specs=P("blk", None, cols, None),
        check_vma=False,
    )
```

time: 536 us -> 482 us (0.90); the launches traced: 534 us -> 473 us
  waiting for transfers between devices: 401 us -> 324 us
  matrix products: 82.6 us -> 91.5 us
  other arithmetic: 6.34 us -> 12.6 us
    all_gather x1, waiting for transfers between devices: 249 us -> 46.3 us  [shards(): rows_a = lax.all_gather(masked_a, 'x', axis=0, tiled=True)]
    ppermute x0 -> x2, waiting for transfers between devices: none -> 70.8 us  [the longest x1 63.9 us: shards(): other_b = lax.ppermute(masked_b, 'ylo', [(0, 1), (1, 0)])]
    reduce_scatter x1 -> x2, waiting for transfers between devices: 152 us -> 207 us  [shards(): lax.psum_scatter(stacked, 'blk', scatter_dimension=0, tiled=True)]
    all_gather x1, local copies, waits for them, and re-layouts: 24.6 us -> 12.6 us  [shards(): rows_a = lax.all_gather(masked_a, 'x', axis=0, tiled=True)]
    dot_general x1 -> x4, matrix products: 82.6 us -> 91.5 us  [shards(): jnp.dot(flat_a, src[:, c * step:(c + 1) * step], precision=lax.Precision....]
    unnamed x9 -> x20, local copies, waits for them, and re-layouts: 2.67 us -> 11.4 us
    concatenate x0 -> x3, other arithmetic: none -> 5.45 us  [the longest x2 4.47 us: shards(): stacked = jnp.concatenate(parts, axis=0)]
  transfers between devices with their start and end apart: 2 -> 5, of which waited for: 2 -> 5; matrix products, arithmetic and copies ran while one was open for 1% -> 13% of each run, Pallas kernels for 0% -> 0%
where the time goes in v1:
time: 482 us; the launch traced here: 473 us
  waiting for transfers between devices  324 us (67%)
  matrix products  91.5 us (19%)
  local copies, waits for them, and re-layouts  27.2 us (6%)
  between operations  13.7 us (3%)
  other arithmetic  12.6 us (3%)
    reduce_scatter x2, waiting for transfers between devices, shards(): lax.psum_scatter(stacked, 'blk', scatter_dimension=0, tiled=True)  207 us
    dot_general x4, matrix products, shards(): jnp.dot(flat_a, src[:, c * step:(c + 1) * step], precision=lax.Precision....  91.5 us
    ppermute x1, waiting for transfers between devices, shards(): other_b = lax.ppermute(masked_b, 'ylo', [(0, 1), (1, 0)])  63.9 us
    all_gather x1, waiting for transfers between devices, shards(): rows_a = lax.all_gather(masked_a, 'x', axis=0, tiled=True)  46.3 us
    all_gather x1, local copies, waits for them, and re-layouts, shards(): rows_a = lax.all_gather(masked_a, 'x', axis=0, tiled=True)  12.6 us
    unnamed x20, local copies, waits for them, and re-layouts  11.4 us
  transfers between devices with their start and end apart: 5, of which 5 were waited for; matrix products, arithmetic and copies ran while one was open for 13% of the time, Pallas kernels for 0%

profile of v1, /device:TPU:24, one launch (start us, length us, event | category | flops | bytes accessed | tf_op | source)
XLA Modules:
  0.0 472.5 jit_solution(14940680039062148186)
XLA Ops:
  7.2 3.8 broadcast_multiply_fusion.1
  11.8 2.6 broadcast_multiply_fusion
  14.4 0.8 collective-permute-start
  15.6 2.0 fusion
  17.5 3.0 copy.47
  20.6 63.9 %collective-permute-done = f32[12,128,4,128]{3,2,1,0:T(4,128)} collective-permute-done((f32[12,128,4,128]{3,2,1,0:T(4,128)S(1)}, f32[12,128,4,128]{3,2,1,0:T(4,128)}, u32[]{:S(2)}, u32[]{:S(2)}) %collective-permute-start) | collective-permute-done | bytes 3145760 | tf_op jit(solution)/shard_map/ppermute | solution.py:27
  84.4 2.2 copy.55
  86.9 1.7 copy.48
  88.7 46.3 %all-gather.2.cloned.1.call-done = f32[16,128,12,128]{3,1,2,0:T(8,128)} async-done(((f32[4,128,12,128]{3,1,2,0:T(8,128)}), f32[16,128,12,128]{3,1,2,0:T(8,128)}) %all-gather.2.cloned.1.call-update) | async-done | bytes 12582928 | tf_op jit(solution)/shard_map/all_gather | solution.py:26
  135.0 12.6 %copy.24 = f32[16,128,12,128]{1,3,2,0:T(8,128)} copy(f32[16,128,12,128]{3,1,2,0:T(8,128)} %all-gather.2.cloned.1.call-done) | data formatting | bytes 25165824 | tf_op jit(solution)/shard_map/all_gather | solution.py:26
  147.6 24.6 %fusion.3 = f32[16,128,2,128]{3,1,2,0:T(8,128)S(1)} fusion(f32[16,128,1536,1]{1,2,3,0:T(8,128)} %bitcast.48, f32[2,128,1536,1]{2,1,0,3:T(8,128)S(1)} %bitcast.56), kind=kOutput, calls=%fused_computation.12 | convolution fusion | flops 9663676416 | bytes 16252928 | tf_op jit(solution)/shard_map/dot_general | solution.py:40
  172.2 20.9 %fusion.2 = f32[16,128,2,128]{3,1,2,0:T(8,128)S(1)} fusion(f32[16,128,1536,1]{1,2,3,0:T(8,128)S(1)} %bitcast.51, f32[2,128,1536,1]{2,1,0,3:T(8,128)S(1)} %bitcast.55), kind=kOutput, calls=%fused_computation.11 | convolution fusion | flops 9663676416 | bytes 16252928 | tf_op jit(solution)/shard_map/dot_general | solution.py:40
  193.1 2.2 pad_maximum_fusion
  195.4 1.3 copy-done.1
  196.7 1.7 copy.49
  198.8 22.9 %fusion.5 = f32[16,128,2,128]{3,1,2,0:T(8,128)S(1)} fusion(f32[16,128,1536,1]{1,2,3,0:T(8,128)} %bitcast.49, f32[2,128,1536,1]{2,1,0,3:T(8,128)S(1)} %bitcast.58), kind=kOutput, calls=%fused_computation.14 | convolution fusion | flops 9663676416 | bytes 16252928 | tf_op jit(solution)/shard_map/dot_general | solution.py:40
  221.8 23.1 %fusion.4 = f32[16,128,2,128]{3,1,2,0:T(8,128)S(1)} fusion(f32[16,128,1536,1]{1,2,3,0:T(8,128)} %bitcast.50, f32[2,128,1536,1]{2,1,0,3:T(8,128)S(1)} %bitcast.57), kind=kOutput, calls=%fused_computation.13 | convolution fusion | flops 9663676416 | bytes 16252928 | tf_op jit(solution)/shard_map/dot_general | solution.py:40
  244.9 2.2 pad_maximum_fusion.1
  247.2 76.2 %reduce-scatter.3.cloned.1.call-done = f32[1,128,2,128]{3,1,2,0:T(8,128)} async-done(((f32[32,128,2,128]{3,1,2,0:T(8,128)}), f32[1,128,2,128]{3,1,2,0:T(8,128)}) %reduce-scatter.3.cloned.1.call-update) | async-done | bytes 131088 | tf_op jit(solution)/shard_map/reduce_scatter | solution.py:48
  323.4 130.4 %reduce-scatter.5.cloned.1.call-done = f32[1,128,2,128]{3,1,2,0:T(8,128)} async-done(((f32[32,128,2,128]{3,1,2,0:T(8,128)}), f32[1,128,2,128]{3,1,2,0:T(8,128)}) %reduce-scatter.5.cloned.1.call-update) | async-done | bytes 131088 | tf_op jit(solution)/shard_map/reduce_scatter | solution.py:48
  453.8 1.0 pad_maximum_fusion.2
  454.8 2.8 collective-permute-start.1
  457.7 6.9 %collective-permute-done.1 = f32[1,128,4,128]{3,1,2,0:T(8,128)S(1)} collective-permute-done((f32[1,128,4,128]{3,1,2,0:T(8,128)S(1)}, f32[1,128,4,128]{3,1,2,0:T(8,128)S(1)}, u32[]{:S(2)}, u32[]{:S(2)}) %collective-permute-start.1) | collective-permute-done | bytes 262176 | tf_op jit(solution)/shard_map/ppermute | solution.py:50
  464.7 0.9 copy.34
  (27 shorter events, 2.7 us)
Async XLA Ops:
  6.5 128.4 %all-gather.2.cloned.1.call-start = ((), (), s32[]{:S(2)}) async-start(), calls=%async_computation.2 | async-start | bytes 15728640 | tf_op jit(solution)/shard_map/all_gather | solution.py:26
  11.0 0.7 copy-start.5
  11.0 312.4 %reduce-scatter.3.cloned.1.call-start = ((), (), s32[]{:S(2)}) async-start(), calls=%async_computation.3 | async-start | bytes 4325376 | tf_op jit(solution)/shard_map/reduce_scatter | solution.py:48
  14.4 70.0 %collective-permute-start = (f32[12,128,4,128]{3,2,1,0:T(4,128)S(1)}, f32[12,128,4,128]{3,2,1,0:T(4,128)}, u32[]{:S(2)}, u32[]{:S(2)}) collective-permute-start(f32[12,128,4,128]{3,2,1,0:T(4,128)S(1)} %broadcast_multiply_fusion), channel_id=1, source_target_pairs={{0,4},{4,0},{1,5},{5,1},{2,6},{6,2},{3,7},{7,3},{8,12},{12,8},{9,1... | collective-permute-start | bytes 9437192 | tf_op jit(solution)/shard_map/ppermute | solution.py:27
  88.7 58.9 %copy-start.3 = (f32[1536,256]{0,1:T(8,128)S(1)}, f32[1536,256]{0,1:T(8,128)}, u32[]{:S(2)}) copy-start(f32[1536,256]{0,1:T(8,128)} %copy.48) | copy-start | bytes 4718596
  147.6 24.6 %copy-start = (f32[16,128,12,128]{1,3,2,0:T(8,128)S(1)}, f32[16,128,12,128]{1,3,2,0:T(8,128)}, u32[]{:S(2)}) copy-start(f32[16,128,12,128]{1,3,2,0:T(8,128)} %copy.24) | copy-start | bytes 37748740
  147.6 24.6 %copy-start.2 = (f32[1536,256]{0,1:T(8,128)S(1)}, f32[1536,256]{0,1:T(8,128)}, u32[]{:S(2)}) copy-start(f32[1536,256]{0,1:T(8,128)} %copy.47) | copy-start | bytes 4718596
  195.3 1.4 copy-start.1
  195.3 258.5 %reduce-scatter.5.cloned.1.call-start = ((), (), s32[]{:S(2)}) async-start(), calls=%async_computation.4 | async-start | bytes 4325376 | tf_op jit(solution)/shard_map/reduce_scatter | solution.py:48
  198.8 23.0 %copy-start.4 = (f32[1536,256]{0,1:T(8,128)S(1)}, f32[1536,256]{0,1:T(8,128)}, u32[]{:S(2)}) copy-start(f32[1536,256]{0,1:T(8,128)} %copy.49) | copy-start | bytes 4718596
  247.2 210.5 %copy-start.6 = (s32[1,4]{1,0:T(1,128)S(1)}, s32[1,4]{1,0:T(1,128)}, u32[]{:S(2)}) copy-start(s32[1,4]{1,0:T(1,128)} %param.9) | copy-start | bytes 52
  454.8 9.8 %collective-permute-start.1 = (f32[1,128,4,128]{3,1,2,0:T(8,128)S(1)}, f32[1,128,4,128]{3,1,2,0:T(8,128)S(1)}, u32[]{:S(2)}, u32[]{:S(2)}) collective-permute-start(f32[1,128,4,128]{3,1,2,0:T(8,128)S(1)} %pad_maximum_fusion.2), channel_id=1, source_target_pairs={{0,0},{1,1},{2,2},{3,3},{4,132},{5,133},{6,134},{7,135},{8,8},{9,9... | collective-permute-start | bytes 786440 | tf_op jit(solution)/shard_map/ppermute | solution.py:50
Sparse Core Ops, SparseCore 0:
  11.2 123.7 all-gather.1
  195.4 127.9 reduce-scatter.2
  327.7 126.1 reduce-scatter.4

commit v2 on v1

v2 whole, which is shorter than its diff:
```python
import jax
import jax.numpy as jnp
from jax import lax
from jax.sharding import Mesh
from jax.sharding import PartitionSpec as P

AXES = ("yhi", "z", "core", "ylo", "x")


def owner_perm(yhis, zs, cores, ylos, xs):
    def linear(yhi, z, c, ylo, x):
        return (((yhi * zs + z) * cores + c) * ylos + ylo) * xs + x

    half = yhis * zs * cores // ylos
    pairs = []
    for yhi in range(yhis):
        for z in range(zs):
            for c in range(cores):
                for ylo in range(ylos):
                    for x in range(xs):
                        t = yhis * z + yhi
                        dst_blk = half * ylo + t
                        dyhi, rest = divmod(dst_blk, zs * cores)
                        dz, dc = divmod(rest, cores)
                        pairs.append((linear(yhi, z, c, ylo, x), linear(dyhi, dz, dc, ylo ^ c, x)))
    return pairs


def shards(a_blocks, a_mask, b_blocks, b_mask, c_mask, *, perm):
    masked_a = a_blocks * a_mask.astype(jnp.float32)[:, None, :, None]
    masked_b = b_blocks * b_mask.astype(jnp.float32)[:, None, :, None]
    rows_a = lax.all_gather(masked_a, "x", axis=0, tiled=True)
    other_b = lax.ppermute(masked_b, "ylo", [(0, 1), (1, 0)])
    rows = rows_a.shape[0] * rows_a.shape[1]
    depth = rows_a.shape[2] * rows_a.shape[3]
    flat_a = rows_a.reshape(rows, depth)
    side = masked_b.shape[3]
    width = masked_b.shape[2] * side
    both_b = jnp.stack([masked_b.reshape(depth, width), other_b.reshape(depth, width)])
    core = lax.axis_index("core")
    keep_b = lax.dynamic_index_in_dim(both_b, core, 0, keepdims=False)
    send_b = lax.dynamic_index_in_dim(both_b, 1 - core, 0, keepdims=False)
    shape = (rows_a.shape[0], rows_a.shape[1], masked_b.shape[2], side)

    def product(src):
        part = jnp.dot(flat_a, src, precision=lax.Precision.HIGHEST, preferred_element_type=jnp.float32)
        return part.reshape(shape)

    sent = lax.ppermute(product(send_b), "core", [(0, 1), (1, 0)])
    (kept,) = lax.optimization_barrier((product(keep_b),))
    summed = kept + sent
    summed = lax.psum_scatter(summed, "z", scatter_dimension=0, tiled=True)
    owned = lax.psum_scatter(summed, "yhi", scatter_dimension=0, tiled=True)
    owned = lax.ppermute(owned, AXES, perm)
    return owned * c_mask.astype(jnp.float32)[:, None, :, None]


def solution(mesh):
    blk = mesh.shape["blk"]
    col = mesh.shape["col"]
    yhis, cores, xs = 2, 2, 4
    zs = blk // (yhis * cores)
    ylos = col // xs
    sub = Mesh(mesh.devices.reshape(yhis, zs, cores, ylos, xs), AXES)
    perm = owner_perm(yhis, zs, cores, ylos, xs)
    rows = ("yhi", "z", "core")
    cols = ("ylo", "x")

    def body(a_blocks, a_mask, b_blocks, b_mask, c_mask):
        return shards(a_blocks, a_mask, b_blocks, b_mask, c_mask, perm=perm)

    return jax.shard_map(
        body,
        mesh=sub,
        in_specs=(
            P(cols, None, rows, None),
            P(cols, rows),
            P(rows, None, cols, None),
            P(rows, cols),
            P(rows, cols),
        ),
        out_specs=P(rows, None, cols, None),
        check_vma=False,
    )
```

time: 482 us -> 341 us (0.71); the launches traced: 473 us -> 338 us
  waiting for transfers between devices: 324 us -> 184 us
  local copies, waits for them, and re-layouts: 27.2 us -> 37.5 us
    reduce_scatter x2, waiting for transfers between devices: 207 us -> 77.4 us  [the longest x1 56.6 us: shards(): summed = lax.psum_scatter(summed, 'z', scatter_dimension=0, tiled=True)]
    dynamic_slice x0 -> x3, local copies, waits for them, and re-layouts: none -> 11.3 us  [the longest x2 8.85 us: shards(): send_b = lax.dynamic_index_in_dim(both_b, 1 - core, 0, keepdims=False)]
    all_gather x1, waiting for transfers between devices: 46.3 us -> 36.4 us  [shards(): rows_a = lax.all_gather(masked_a, 'x', axis=0, tiled=True)]
    another operation x0 -> x3, local copies, waits for them, and re-layouts: none -> 8.17 us  [shards(): jnp.stack([masked_b.reshape(depth, width), other_b.reshape(depth, width)])]
    unnamed x20 -> x5, local copies, waits for them, and re-layouts: 11.4 us -> 4.44 us
    concatenate x3 -> x0, other arithmetic: 5.45 us -> none  [the longest x2 4.47 us: shards(): stacked = jnp.concatenate(parts, axis=0)]
    add x0 -> x1, other arithmetic: none -> 4.89 us  [shards(): summed = kept + sent]
    dot_general x4 -> x2, matrix products: 91.5 us -> 88.2 us  [product(): jnp.dot(flat_a, src, precision=lax.Precision.HIGHEST, preferred_element_t...]
  transfers between devices with their start and end apart: 5 -> 6, of which waited for: 5 -> 5; matrix products, arithmetic and copies ran while one was open for 13% -> 21% of each run, Pallas kernels for 0% -> 0%
where the time goes in v2:
time: 341 us; the launch traced here: 338 us
  waiting for transfers between devices  184 us (54%)
  matrix products  88.2 us (26%)
  local copies, waits for them, and re-layouts  37.5 us (11%)
  between operations  13.2 us (4%)
  other arithmetic  12.1 us (4%)
    dot_general x2, matrix products, product(): jnp.dot(flat_a, src, precision=lax.Precision.HIGHEST, preferred_element_t...  88.2 us
    ppermute x1, waiting for transfers between devices, shards(): other_b = lax.ppermute(masked_b, 'ylo', [(0, 1), (1, 0)])  62.5 us
    reduce_scatter x1, waiting for transfers between devices, shards(): summed = lax.psum_scatter(summed, 'z', scatter_dimension=0, tiled=True)  56.6 us
    all_gather x1, waiting for transfers between devices, shards(): rows_a = lax.all_gather(masked_a, 'x', axis=0, tiled=True)  36.4 us
    reduce_scatter x1, waiting for transfers between devices, shards(): owned = lax.psum_scatter(summed, 'yhi', scatter_dimension=0, tiled=True)  20.8 us
    all_gather x1, local copies, waits for them, and re-layouts, shards(): rows_a = lax.all_gather(masked_a, 'x', axis=0, tiled=True)  12.6 us
    dynamic_slice x2, local copies, waits for them, and re-layouts, shards(): send_b = lax.dynamic_index_in_dim(both_b, 1 - core, 0, keepdims=False)  8.85 us
    another operation x3, local copies, waits for them, and re-layouts, shards(): jnp.stack([masked_b.reshape(depth, width), other_b.reshape(depth, width)])  8.17 us
  transfers between devices with their start and end apart: 6, of which 5 were waited for; matrix products, arithmetic and copies ran while one was open for 21% of the time, Pallas kernels for 0%

profile of v2, /device:TPU:24, one launch (start us, length us, event | category | flops | bytes accessed | tf_op | source)
XLA Modules:
  0.0 338.0 jit_solution(6130511781708007517)
XLA Ops:
  6.5 0.7 convert_element_type.9
  7.2 3.8 %broadcast_multiply_fusion.1 = f32[4,128,12,128]{3,1,2,0:T(8,128)} fusion(f32[4,128,12,128]{3,1,2,0:T(8,128)} %param.5, f32[4,12]{1,0:T(4,128)S(1)} %convert_element_type.9), kind=kLoop, calls=%fused_computation.1 | loop fusion | flops 786432 | bytes 6291648 | tf_op jit(solution)/shard_map/mul | solution.py:30
  11.1 0.6 copy-done
  11.7 0.1 copy.19
  11.8 2.6 broadcast_multiply_fusion
  14.4 0.8 collective-permute-start
  15.3 2.9 stack_reshape.6
  18.1 3.8 %constant_dynamic-update-slice_fusion.1 = f32[2,1536,512]{2,1,0:T(8,128)} fusion(f32[1,1536,512]{2,1,0:T(8,128)} %stack_reshape.6), kind=kLoop, calls=%fused_computation.4 | loop fusion | bytes 6291456
  22.0 62.5 %collective-permute-done = f32[12,128,4,128]{3,2,1,0:T(4,128)} collective-permute-done((f32[12,128,4,128]{3,2,1,0:T(4,128)S(1)}, f32[12,128,4,128]{3,2,1,0:T(4,128)}, u32[]{:S(2)}, u32[]{:S(2)}) %collective-permute-start) | collective-permute-done | bytes 3145760 | tf_op jit(solution)/shard_map/ppermute | solution.py:33
  84.5 3.3 stack_reshape.7
  87.8 2.0 constant_dynamic-update-slice_fusion
  89.8 5.2 %constant_dynamic-slice_fusion = (f32[1,1536,512]{2,1,0:T(8,128)}, f32[1,1536,512]{2,1,0:T(8,128)S(1)}) fusion(f32[2,1536,512]{2,1,0:T(8,128)} %constant_dynamic-update-slice_fusion, s32[]{:T(128)S(6)} %select_n.8, s32[]{:T(128)S(6)} %select_n.7), kind=kLoop, calls=%fused_computation.6 | loop fusion | bytes 12582920 | tf_op jit(solution)/shard_map/jit(dynamic_index_in_dim)/dynamic_slice | solution.py:42
  95.0 3.6 %copy.22 = f32[1,1536,512]{1,2,0:T(8,128)} copy(f32[1,1536,512]{2,1,0:T(8,128)} %get-tuple-element.5) | data formatting | bytes 6291456 | tf_op jit(solution)/shard_map/jit(dynamic_index_in_dim)/dynamic_slice | solution.py:42
  98.6 36.4 %all-gather.2.cloned.1.call-done = f32[16,128,12,128]{3,1,2,0:T(8,128)} async-done(((f32[4,128,12,128]{3,1,2,0:T(8,128)}), f32[16,128,12,128]{3,1,2,0:T(8,128)}) %all-gather.2.cloned.1.call-update) | async-done | bytes 12582928 | tf_op jit(solution)/shard_map/all_gather | solution.py:32
  135.0 12.6 %copy.18 = f32[16,128,12,128]{1,3,2,0:T(8,128)} copy(f32[16,128,12,128]{3,1,2,0:T(8,128)} %all-gather.2.cloned.1.call-done) | data formatting | bytes 25165824 | tf_op jit(solution)/shard_map/all_gather | solution.py:32
  147.6 43.6 %fusion.1 = f32[16,128,4,128]{3,1,2,0:T(8,128)} fusion(f32[16,128,1536,1]{1,2,3,0:T(8,128)} %bitcast.26, f32[4,128,1536,1]{2,1,0,3:T(8,128)} %bitcast.28), kind=kOutput, calls=%fused_computation.9 | convolution fusion | flops 19327352832 | bytes 19922944 | tf_op jit(solution)/shard_map/dot_general | solution.py:46
  191.2 2.4 copy.20
  193.7 44.5 %fusion = f32[16,128,4,128]{3,1,2,0:T(8,128)S(1)} fusion(f32[16,128,1536,1]{1,2,3,0:T(8,128)} %bitcast.27, f32[4,128,1536,1]{2,1,0,3:T(8,128)} %bitcast.29), kind=kOutput, calls=%fused_computation.8 | convolution fusion | flops 19327352832 | bytes 19922944 | tf_op jit(solution)/shard_map/dot_general | solution.py:46
  238.2 4.9 %add.17 = f32[16,128,4,128]{3,1,2,0:T(8,128)} add(f32[16,128,4,128]{3,1,2,0:T(8,128)S(1)} %fusion, f32[16,128,4,128]{3,1,2,0:T(8,128)} %collective-permute-done.1) | non-fusion elementwise | flops 1048576 | bytes 12582912 | tf_op jit(solution)/shard_map/add | solution.py:51
  243.2 56.6 %reduce-scatter.3.cloned.1.call-done = f32[2,128,4,128]{3,1,2,0:T(8,128)} async-done(((f32[16,128,4,128]{3,1,2,0:T(8,128)}), f32[2,128,4,128]{3,1,2,0:T(8,128)}) %reduce-scatter.3.cloned.1.call-update) | async-done | bytes 524304 | tf_op jit(solution)/shard_map/reduce_scatter | solution.py:52
  299.8 20.8 %reduce-scatter.5.cloned.1.call-done = f32[1,128,4,128]{3,1,2,0:T(8,128)} async-done(((f32[2,128,4,128]{3,1,2,0:T(8,128)}), f32[1,128,4,128]{3,1,2,0:T(8,128)}) %reduce-scatter.5.cloned.1.call-update) | async-done | bytes 262160 | tf_op jit(solution)/shard_map/reduce_scatter | solution.py:53
  320.6 1.9 collective-permute-start.2
  322.5 8.0 %collective-permute-done.2 = f32[1,128,4,128]{3,1,2,0:T(8,128)S(1)} collective-permute-done((f32[1,128,4,128]{3,1,2,0:T(8,128)}, f32[1,128,4,128]{3,1,2,0:T(8,128)S(1)}, u32[]{:S(2)}, u32[]{:S(2)}) %collective-permute-start.2) | collective-permute-done | bytes 262176 | tf_op jit(solution)/shard_map/ppermute | solution.py:54
  330.6 0.9 copy.24
  (14 shorter events, 0.2 us)
Async XLA Ops:
  6.5 128.5 %all-gather.2.cloned.1.call-start = ((), (), s32[]{:S(2)}) async-start(), calls=%async_computation.2 | async-start | bytes 15728640 | tf_op jit(solution)/shard_map/all_gather | solution.py:32
  11.0 0.7 copy-start
  11.1 288.7 %reduce-scatter.3.cloned.1.call-start = ((), (), s32[]{:S(2)}) async-start(), calls=%async_computation.3 | async-start | bytes 4718592 | tf_op jit(solution)/shard_map/reduce_scatter | solution.py:52
  14.4 70.0 %collective-permute-start = (f32[12,128,4,128]{3,2,1,0:T(4,128)S(1)}, f32[12,128,4,128]{3,2,1,0:T(4,128)}, u32[]{:S(2)}, u32[]{:S(2)}) collective-permute-start(f32[12,128,4,128]{3,2,1,0:T(4,128)S(1)} %broadcast_multiply_fusion), channel_id=1, source_target_pairs={{0,4},{4,0},{1,5},{5,1},{2,6},{6,2},{3,7},{7,3},{8,12},{12,8},{9,1... | collective-permute-start | bytes 9437192 | tf_op jit(solution)/shard_map/ppermute | solution.py:33
  191.2 47.0 %collective-permute-start.1 = (f32[16,128,4,128]{3,1,2,0:T(8,128)}, f32[16,128,4,128]{3,1,2,0:T(8,128)}, u32[]{:S(2)}, u32[]{:S(2)}) collective-permute-start(f32[16,128,4,128]{3,1,2,0:T(8,128)} %fusion.1), channel_id=1, source_target_pairs={{0,8},{8,0},{1,9},{9,1},{2,10},{10,2},{3,11},{11,3},{4,12},{12,4},... | collective-permute-start | bytes 12582920 | tf_op jit(solution)/shard_map/ppermute | solution.py:49
  243.1 79.4 %copy-start.1 = (s32[1,4]{1,0:T(1,128)S(1)}, s32[1,4]{1,0:T(1,128)}, u32[]{:S(2)}) copy-start(s32[1,4]{1,0:T(1,128)} %param.9) | copy-start | bytes 52
  243.2 77.4 %reduce-scatter.5.cloned.1.call-start = ((), (), s32[]{:S(2)}) async-start(), calls=%async_computation.4 | async-start | bytes 786432 | tf_op jit(solution)/shard_map/reduce_scatter | solution.py:53
  320.6 10.0 %collective-permute-start.2 = (f32[1,128,4,128]{3,1,2,0:T(8,128)}, f32[1,128,4,128]{3,1,2,0:T(8,128)S(1)}, u32[]{:S(2)}, u32[]{:S(2)}) collective-permute-start(f32[1,128,4,128]{3,1,2,0:T(8,128)} %reduce-scatter.5.cloned.1.call-done), channel_id=1, source_target_pairs={{0,0},{1,1},{2,2},{3,3},{4,132},{5,133},{6,134},{7,135},{8,4},{9,5... | collective-permute-start | bytes 786440 | tf_op jit(solution)/shard_map/ppermute | solution.py:54
Sparse Core Ops, SparseCore 0:
  11.2 123.7 all-gather.1
  243.3 56.4 reduce-scatter.2
  302.3 18.2 reduce-scatter.4

commit v3 on v2

--- a/solution.py
+++ b/solution.py
@@ -29,21 +29,20 @@
 def shards(a_blocks, a_mask, b_blocks, b_mask, c_mask, *, perm):
     masked_a = a_blocks * a_mask.astype(jnp.float32)[:, None, :, None]
     masked_b = b_blocks * b_mask.astype(jnp.float32)[:, None, :, None]
-    rows_a = lax.all_gather(masked_a, "x", axis=0, tiled=True)
+    rows_a = lax.all_gather(masked_a.transpose(0, 2, 3, 1), "x", axis=0, tiled=True)
     other_b = lax.ppermute(masked_b, "ylo", [(0, 1), (1, 0)])
-    rows = rows_a.shape[0] * rows_a.shape[1]
-    depth = rows_a.shape[2] * rows_a.shape[3]
-    flat_a = rows_a.reshape(rows, depth)
+    depth = rows_a.shape[1] * rows_a.shape[2]
+    flat_a = rows_a.reshape(rows_a.shape[0], depth, rows_a.shape[3])
     side = masked_b.shape[3]
     width = masked_b.shape[2] * side
     both_b = jnp.stack([masked_b.reshape(depth, width), other_b.reshape(depth, width)])
     core = lax.axis_index("core")
     keep_b = lax.dynamic_index_in_dim(both_b, core, 0, keepdims=False)
     send_b = lax.dynamic_index_in_dim(both_b, 1 - core, 0, keepdims=False)
-    shape = (rows_a.shape[0], rows_a.shape[1], masked_b.shape[2], side)
+    shape = (rows_a.shape[0], rows_a.shape[3], masked_b.shape[2], side)
 
     def product(src):
-        part = jnp.dot(flat_a, src, precision=lax.Precision.HIGHEST, preferred_element_type=jnp.float32)
+        part = jnp.einsum("tka,kn->tan", flat_a, src, precision=lax.Precision.HIGH, preferred_element_type=jnp.float32)
         return part.reshape(shape)
 
     sent = lax.ppermute(product(send_b), "core", [(0, 1), (1, 0)])

time: 341 us -> 288 us (0.84)
  matrix products: 88.2 us -> 48.2 us
  local copies, waits for them, and re-layouts: 37.5 us -> 27.2 us
    dot_general x2, matrix products: 88.2 us -> 48.2 us  [product(): jnp.einsum('tka,kn->tan', flat_a, src, precision=lax.Precision.HIGH, pref...]
    all_gather x1 -> x0, local copies, waits for them, and re-layouts: 12.6 us -> none  [shards(): rows_a = lax.all_gather(masked_a, 'x', axis=0, tiled=True)]
    mul x1 -> x0, other arithmetic: 3.82 us -> none  [shards(): masked_a = a_blocks * a_mask.astype(jnp.float32)[:, None, :, None]]
    unnamed x5 -> x8, local copies, waits for them, and re-layouts: 4.44 us -> 6.83 us
  transfers between devices with their start and end apart: 6 -> 6, of which waited for: 5 -> 5; matrix products, arithmetic and copies ran while one was open for 21% -> 17% of each run, Pallas kernels for 0% -> 0%
where the time goes in v3:
time: 288 us; the launch traced here: 285 us
  waiting for transfers between devices  184 us (64%)
  matrix products  48.2 us (17%)
  local copies, waits for them, and re-layouts  27.2 us (9%)
  between operations  13.2 us (5%)
  other arithmetic  9.54 us (3%)
    ppermute x1, waiting for transfers between devices, shards(): other_b = lax.ppermute(masked_b, 'ylo', [(0, 1), (1, 0)])  62.5 us
    reduce_scatter x1, waiting for transfers between devices, shards(): summed = lax.psum_scatter(summed, 'z', scatter_dimension=0, tiled=True)  56.6 us
    dot_general x2, matrix products, product(): jnp.einsum('tka,kn->tan', flat_a, src, precision=lax.Precision.HIGH, pref...  48.2 us
    all_gather x1, waiting for transfers between devices, shards(): lax.all_gather(masked_a.transpose(0, 2, 3, 1), 'x', axis=0, tiled=True)  36.4 us
    reduce_scatter x1, waiting for transfers between devices, shards(): owned = lax.psum_scatter(summed, 'yhi', scatter_dimension=0, tiled=True)  20.8 us
    dynamic_slice x2, local copies, waits for them, and re-layouts, shards(): send_b = lax.dynamic_index_in_dim(both_b, 1 - core, 0, keepdims=False)  8.86 us
    another operation x3, local copies, waits for them, and re-layouts, shards(): jnp.stack([masked_b.reshape(depth, width), other_b.reshape(depth, width)])  8.18 us
    ppermute x1, waiting for transfers between devices, shards(): owned = lax.ppermute(owned, AXES, perm)  8.03 us
  transfers between devices with their start and end apart: 6, of which 5 were waited for; matrix products, arithmetic and copies ran while one was open for 17% of the time, Pallas kernels for 0%

profile of v3, /device:TPU:24, one launch (start us, length us, event | category | flops | bytes accessed | tf_op | source)
XLA Modules:
  0.0 285.2 jit_solution(819072070286825972)
XLA Ops:
  6.5 2.4 copy.18
  9.0 1.9 multiply_bitcast_fusion
  11.0 0.6 copy-done.1
  11.6 0.1 copy.19
  11.7 2.6 broadcast_multiply_fusion
  14.3 0.8 collective-permute-start
  15.1 2.9 %stack_reshape.6 = f32[1,1536,512]{2,1,0:T(8,128)} reshape(f32[12,128,4,128]{3,2,1,0:T(4,128)S(1)} %broadcast_multiply_fusion) | data formatting | bytes 6291456 | tf_op jit(solution)/shard_map/stack;reshape | solution.py:38
  18.0 3.8 %constant_dynamic-update-slice_fusion.1 = f32[2,1536,512]{2,1,0:T(8,128)} fusion(f32[1,1536,512]{2,1,0:T(8,128)} %stack_reshape.6), kind=kLoop, calls=%fused_computation.4 | loop fusion | bytes 6291456
  21.8 62.5 %collective-permute-done = f32[12,128,4,128]{3,2,1,0:T(4,128)} collective-permute-done((f32[12,128,4,128]{3,2,1,0:T(4,128)S(1)}, f32[12,128,4,128]{3,2,1,0:T(4,128)}, u32[]{:S(2)}, u32[]{:S(2)}) %collective-permute-start) | collective-permute-done | bytes 3145760 | tf_op jit(solution)/shard_map/ppermute | solution.py:33
  84.3 3.3 %stack_reshape.7 = f32[1,1536,512]{2,1,0:T(8,128)S(1)} reshape(f32[12,128,4,128]{3,2,1,0:T(4,128)} %collective-permute-done) | data formatting | bytes 6291456 | tf_op jit(solution)/shard_map/stack;reshape | solution.py:38
  87.7 2.0 constant_dynamic-update-slice_fusion
  89.6 5.3 %constant_dynamic-slice_fusion = (f32[1,1536,512]{2,1,0:T(8,128)}, f32[1,1536,512]{2,1,0:T(8,128)S(1)}) fusion(f32[2,1536,512]{2,1,0:T(8,128)} %constant_dynamic-update-slice_fusion, s32[]{:T(128)S(6)} %select_n.8, s32[]{:T(128)S(6)} %select_n.7), kind=kLoop, calls=%fused_computation.6 | loop fusion | bytes 12582920 | tf_op jit(solution)/shard_map/jit(dynamic_index_in_dim)/dynamic_slice | solution.py:41
  94.9 3.6 %copy.22 = f32[1,1536,512]{1,2,0:T(8,128)} copy(f32[1,1536,512]{2,1,0:T(8,128)} %get-tuple-element.5) | data formatting | bytes 6291456 | tf_op jit(solution)/shard_map/jit(dynamic_index_in_dim)/dynamic_slice | solution.py:41
  98.5 36.4 %all-gather.2.cloned.1.call-done = f32[16,12,128,128]{3,2,1,0:T(8,128)} async-done(((f32[4,12,128,128]{3,2,1,0:T(8,128)}), f32[16,12,128,128]{3,2,1,0:T(8,128)}) %all-gather.2.cloned.1.call-update) | async-done | bytes 12582928 | tf_op jit(solution)/shard_map/all_gather | solution.py:32
  134.9 24.3 %fusion.1 = f32[16,128,4,128]{3,1,2,0:T(8,128)} fusion(f32[16,1536,128,1]{2,1,3,0:T(8,128)} %bitcast.30, f32[4,128,1536,1]{2,1,0,3:T(8,128)} %bitcast.28), kind=kOutput, calls=%fused_computation.9 | convolution fusion | flops 9663676416 | bytes 19922944 | tf_op jit(solution)/shard_map/tka,kn->tan/dot_general | solution.py:45
  159.1 2.3 copy.20
  161.5 23.9 %fusion = f32[16,128,4,128]{3,1,2,0:T(8,128)S(1)} fusion(f32[16,1536,128,1]{2,1,3,0:T(8,128)} %bitcast.31, f32[4,128,1536,1]{2,1,0,3:T(8,128)} %bitcast.29), kind=kOutput, calls=%fused_computation.8 | convolution fusion | flops 9663676416 | bytes 19922944 | tf_op jit(solution)/shard_map/tka,kn->tan/dot_general | solution.py:45
  185.4 4.9 %add.17 = f32[16,128,4,128]{3,1,2,0:T(8,128)} add(f32[16,128,4,128]{3,1,2,0:T(8,128)S(1)} %fusion, f32[16,128,4,128]{3,1,2,0:T(8,128)} %collective-permute-done.1) | non-fusion elementwise | flops 1048576 | bytes 12582912 | tf_op jit(solution)/shard_map/add | solution.py:50
  190.4 56.6 %reduce-scatter.3.cloned.1.call-done = f32[2,128,4,128]{3,1,2,0:T(8,128)} async-done(((f32[16,128,4,128]{3,1,2,0:T(8,128)}), f32[2,128,4,128]{3,1,2,0:T(8,128)}) %reduce-scatter.3.cloned.1.call-update) | async-done | bytes 524304 | tf_op jit(solution)/shard_map/reduce_scatter | solution.py:51
  247.0 20.8 %reduce-scatter.5.cloned.1.call-done = f32[1,128,4,128]{3,1,2,0:T(8,128)} async-done(((f32[2,128,4,128]{3,1,2,0:T(8,128)}), f32[1,128,4,128]{3,1,2,0:T(8,128)}) %reduce-scatter.5.cloned.1.call-update) | async-done | bytes 262160 | tf_op jit(solution)/shard_map/reduce_scatter | solution.py:52
  267.8 1.9 collective-permute-start.2
  269.7 8.0 %collective-permute-done.2 = f32[1,128,4,128]{3,1,2,0:T(8,128)S(1)} collective-permute-done((f32[1,128,4,128]{3,1,2,0:T(8,128)}, f32[1,128,4,128]{3,1,2,0:T(8,128)S(1)}, u32[]{:S(2)}, u32[]{:S(2)}) %collective-permute-start.2) | collective-permute-done | bytes 262176 | tf_op jit(solution)/shard_map/ppermute | solution.py:53
  277.7 0.1 broadcast_multiply_fusion.1
  277.8 0.9 copy.24
  (16 shorter events, 0.2 us)
Async XLA Ops:
  6.5 2.4 copy-start
  6.5 128.3 %all-gather.2.cloned.1.call-start = ((), (), s32[]{:S(2)}) async-start(), calls=%async_computation.2 | async-start | bytes 15728640 | tf_op jit(solution)/shard_map/all_gather | solution.py:32
  10.9 0.7 copy-start.1
  10.9 236.0 %reduce-scatter.3.cloned.1.call-start = ((), (), s32[]{:S(2)}) async-start(), calls=%async_computation.3 | async-start | bytes 4718592 | tf_op jit(solution)/shard_map/reduce_scatter | solution.py:51
  14.3 70.0 %collective-permute-start = (f32[12,128,4,128]{3,2,1,0:T(4,128)S(1)}, f32[12,128,4,128]{3,2,1,0:T(4,128)}, u32[]{:S(2)}, u32[]{:S(2)}) collective-permute-start(f32[12,128,4,128]{3,2,1,0:T(4,128)S(1)} %broadcast_multiply_fusion), channel_id=1, source_target_pairs={{0,4},{4,0},{1,5},{5,1},{2,6},{6,2},{3,7},{7,3},{8,12},{12,8},{9,1... | collective-permute-start | bytes 9437192 | tf_op jit(solution)/shard_map/ppermute | solution.py:33
  159.1 26.3 %collective-permute-start.1 = (f32[16,128,4,128]{3,1,2,0:T(8,128)}, f32[16,128,4,128]{3,1,2,0:T(8,128)}, u32[]{:S(2)}, u32[]{:S(2)}) collective-permute-start(f32[16,128,4,128]{3,1,2,0:T(8,128)} %fusion.1), channel_id=1, source_target_pairs={{0,8},{8,0},{1,9},{9,1},{2,10},{10,2},{3,11},{11,3},{4,12},{12,4},... | collective-permute-start | bytes 12582920 | tf_op jit(solution)/shard_map/ppermute | solution.py:48
  190.3 79.4 %copy-start.2 = (s32[1,4]{1,0:T(1,128)S(1)}, s32[1,4]{1,0:T(1,128)}, u32[]{:S(2)}) copy-start(s32[1,4]{1,0:T(1,128)} %param.9) | copy-start | bytes 52
  190.3 77.4 %reduce-scatter.5.cloned.1.call-start = ((), (), s32[]{:S(2)}) async-start(), calls=%async_computation.4 | async-start | bytes 786432 | tf_op jit(solution)/shard_map/reduce_scatter | solution.py:52
  267.8 10.0 %collective-permute-start.2 = (f32[1,128,4,128]{3,1,2,0:T(8,128)}, f32[1,128,4,128]{3,1,2,0:T(8,128)S(1)}, u32[]{:S(2)}, u32[]{:S(2)}) collective-permute-start(f32[1,128,4,128]{3,1,2,0:T(8,128)} %reduce-scatter.5.cloned.1.call-done), channel_id=1, source_target_pairs={{0,0},{1,1},{2,2},{3,3},{4,132},{5,133},{6,134},{7,135},{8,4},{9,5... | collective-permute-start | bytes 786440 | tf_op jit(solution)/shard_map/ppermute | solution.py:53
Sparse Core Ops, SparseCore 0:
  11.0 123.7 all-gather.1
  190.5 56.4 reduce-scatter.2
  249.5 18.2 reduce-scatter.4

commit v4 on v3

v4 whole, which is shorter than its diff:
```python
import jax
import jax.numpy as jnp
from jax import lax
from jax.sharding import Mesh
from jax.sharding import PartitionSpec as P

AXES = ("yhi", "z", "core", "ylo", "x")
K_CHUNKS = 2


def owner_perm(yhis, zs, cores, ylos, xs, flip):
    def linear(yhi, z, c, ylo, x):
        return (((yhi * zs + z) * cores + c) * ylos + ylo) * xs + x

    half = yhis * zs * cores // ylos
    pairs = []
    for yhi in range(yhis):
        for z in range(zs):
            for c in range(cores):
                for ylo in range(ylos):
                    for x in range(xs):
                        t = yhis * z + (yhi ^ flip)
                        dst_blk = half * ylo + t
                        dyhi, rest = divmod(dst_blk, zs * cores)
                        dz, dc = divmod(rest, cores)
                        pairs.append((linear(yhi, z, c, ylo, x), linear(dyhi, dz, dc, ylo ^ c, x)))
    return pairs


def shards(a_blocks, a_mask, b_blocks, b_mask, c_mask, *, perms):
    masked_a = a_blocks * a_mask.astype(jnp.float32)[:, None, :, None]
    masked_b = b_blocks * b_mask.astype(jnp.float32)[:, None, :, None]
    local_a = masked_a.transpose(0, 2, 3, 1)
    other_b = lax.ppermute(masked_b, "ylo", [(0, 1), (1, 0)])
    side = masked_b.shape[3]
    width = masked_b.shape[2] * side
    depth = masked_b.shape[0] * masked_b.shape[1]
    both_b = jnp.stack([masked_b.reshape(depth, width), other_b.reshape(depth, width)])
    core = lax.axis_index("core")
    keep_b = lax.dynamic_index_in_dim(both_b, core, 0, keepdims=False)
    send_b = lax.dynamic_index_in_dim(both_b, 1 - core, 0, keepdims=False)

    step = masked_a.shape[2] // K_CHUNKS
    send_part = keep_part = None
    for c in range(K_CHUNKS):
        rows_a = lax.all_gather(local_a[:, c * step:(c + 1) * step], "x", axis=0, tiled=True)
        flat_a = rows_a.reshape(rows_a.shape[0], step * rows_a.shape[2], rows_a.shape[3])
        lo, hi = c * step * side, (c + 1) * step * side

        def product(src):
            return jnp.einsum("tka,kn->tan", flat_a, src[lo:hi], precision=lax.Precision.HIGH,
                              preferred_element_type=jnp.float32)

        s, k = product(send_b), product(keep_b)
        send_part = s if send_part is None else send_part + s
        keep_part = k if keep_part is None else keep_part + k
    shape = (send_part.shape[0], send_part.shape[1], masked_b.shape[2], side)
    sent = lax.ppermute(send_part.reshape(shape), "core", [(0, 1), (1, 0)])
    (kept,) = lax.optimization_barrier((keep_part.reshape(shape),))
    summed = kept + sent
    summed = lax.psum_scatter(summed, "z", scatter_dimension=0, tiled=True)
    yhi = lax.axis_index("yhi")
    first = lax.dynamic_index_in_dim(summed, yhi, 0, keepdims=True)
    second = lax.dynamic_index_in_dim(summed, 1 - yhi, 0, keepdims=True)
    owned = lax.ppermute(first, AXES, perms[0]) + lax.ppermute(second, AXES, perms[1])
    return owned * c_mask.astype(jnp.float32)[:, None, :, None]


def solution(mesh):
    blk = mesh.shape["blk"]
    col = mesh.shape["col"]
    yhis, cores, xs = 2, 2, 4
    zs = blk // (yhis * cores)
    ylos = col // xs
    sub = Mesh(mesh.devices.reshape(yhis, zs, cores, ylos, xs), AXES)
    perms = [owner_perm(yhis, zs, cores, ylos, xs, flip) for flip in (0, 1)]
    rows = ("yhi", "z", "core")
    cols = ("ylo", "x")

    def body(a_blocks, a_mask, b_blocks, b_mask, c_mask):
        return shards(a_blocks, a_mask, b_blocks, b_mask, c_mask, perms=perms)

    return jax.shard_map(
        body,
        mesh=sub,
        in_specs=(
            P(cols, None, rows, None),
            P(cols, rows),
            P(rows, None, cols, None),
            P(rows, cols),
            P(rows, cols),
        ),
        out_specs=P(rows, None, cols, None),
        check_vma=False,
    )
```

time: 288 us -> 270 us (0.938)
  matrix products: 48.2 us -> 33.6 us
  waiting for transfers between devices: 184 us -> 181 us
    reduce_scatter x1 -> x0, waiting for transfers between devices: 20.8 us -> none  [shards(): owned = lax.psum_scatter(summed, 'yhi', scatter_dimension=0, tiled=True)]
    all_gather x1 -> x2, waiting for transfers between devices: 36.4 us -> 53.9 us  [shards(): lax.all_gather(local_a[:, c * step:(c + 1) * step], 'x', axis=0, tiled=True)]
    dot_general x2 -> x4, matrix products: 48.2 us -> 33.6 us  [product(): jnp.einsum('tka,kn->tan', flat_a, src[lo:hi], precision=lax.Precision.HIG...]
    dynamic_slice x3 -> x1, local copies, waits for them, and re-layouts: 11.2 us -> 1.06 us  [shards(): second = lax.dynamic_index_in_dim(summed, 1 - yhi, 0, keepdims=True)]
    reshape x0 -> x2, local copies, waits for them, and re-layouts: none -> 7.86 us  [the longest x1 5.25 us: shards(): kept, = lax.optimization_barrier((keep_part.reshape(shape),))]
    ppermute x2 -> x3, waiting for transfers between devices: 8.03 us -> 7.14 us  [the longest x1 7.14 us: shards(): lax.ppermute(first, AXES, perms[0]) + lax.ppermute(second, AXES, perms[1])]
    unnamed x8 -> x12, local copies, waits for them, and re-layouts: 6.83 us -> 6.25 us
  transfers between devices with their start and end apart: 6 -> 7, of which waited for: 5 -> 4; matrix products, arithmetic and copies ran while one was open for 17% -> 17% of each run, Pallas kernels for 0% -> 0%
where the time goes in v4:
time: 270 us; the launch traced here: 267 us
  waiting for transfers between devices  181 us (67%)
  matrix products  33.6 us (12%)
  local copies, waits for them, and re-layouts  26.2 us (10%)
  between operations  13.3 us (5%)
  other arithmetic  9.42 us (3%)
  starting transfers between devices  3.51 us (1%)
    ppermute x1, waiting for transfers between devices, shards(): other_b = lax.ppermute(masked_b, 'ylo', [(0, 1), (1, 0)])  62.5 us
    reduce_scatter x1, waiting for transfers between devices, shards(): summed = lax.psum_scatter(summed, 'z', scatter_dimension=0, tiled=True)  56.3 us
    all_gather x2, waiting for transfers between devices, shards(): lax.all_gather(local_a[:, c * step:(c + 1) * step], 'x', axis=0, tiled=True)  53.9 us
    dot_general x4, matrix products, product(): jnp.einsum('tka,kn->tan', flat_a, src[lo:hi], precision=lax.Precision.HIG...  33.6 us
    another operation x3, local copies, waits for them, and re-layouts, shards(): jnp.stack([masked_b.reshape(depth, width), other_b.reshape(depth, width)])  8.17 us
    ppermute x1, waiting for transfers between devices, shards(): lax.ppermute(first, AXES, perms[0]) + lax.ppermute(second, AXES, perms[1])  7.14 us
    add x1, other arithmetic, shards(): summed = kept + sent  6.45 us
    unnamed x12, local copies, waits for them, and re-layouts  6.25 us
  transfers between devices with their start and end apart: 7, of which 4 were waited for; matrix products, arithmetic and copies ran while one was open for 17% of the time, Pallas kernels for 0%

profile of v4, /device:TPU:24, one launch (start us, length us, event | category | flops | bytes accessed | tf_op | source)
XLA Modules:
  0.0 266.5 jit_solution(2727311489535522548)
XLA Ops:
  6.5 2.4 copy.15
  9.2 1.9 fusion.6
  11.2 0.7 all-gather.3.cloned.1.call-update
  12.1 2.6 broadcast_multiply_fusion
  14.7 0.8 collective-permute-start
  15.5 2.9 %stack_reshape.6 = f32[1,1536,512]{2,1,0:T(8,128)} reshape(f32[12,128,4,128]{3,2,1,0:T(4,128)S(1)} %broadcast_multiply_fusion) | data formatting | bytes 6291456 | tf_op jit(solution)/shard_map/stack;reshape | solution.py:38
  18.4 3.8 %constant_dynamic-update-slice_fusion.1 = f32[2,1536,512]{2,1,0:T(8,128)} fusion(f32[1,1536,512]{2,1,0:T(8,128)} %stack_reshape.6), kind=kLoop, calls=%fused_computation.14 | loop fusion | bytes 6291456
  22.3 62.5 %collective-permute-done = f32[12,128,4,128]{3,2,1,0:T(4,128)} collective-permute-done((f32[12,128,4,128]{3,2,1,0:T(4,128)S(1)}, f32[12,128,4,128]{3,2,1,0:T(4,128)}, u32[]{:S(2)}, u32[]{:S(2)}) %collective-permute-start) | collective-permute-done | bytes 3145760 | tf_op jit(solution)/shard_map/ppermute | solution.py:34
  84.7 3.3 %stack_reshape.7 = f32[1,1536,512]{2,1,0:T(8,128)S(1)} reshape(f32[12,128,4,128]{3,2,1,0:T(4,128)} %collective-permute-done) | data formatting | bytes 6291456 | tf_op jit(solution)/shard_map/stack;reshape | solution.py:38
  88.1 2.0 constant_dynamic-update-slice_fusion
  90.0 9.0 %fusion = f32[16,128,512]{2,1,0:T(8,128)} fusion(f32[16,768,128]{2,1,0:T(8,128)} %bitcast.31, f32[2,1536,512]{2,1,0:T(8,128)} %constant_dynamic-update-slice_fusion, s32[]{:T(128)S(6)} %select_n.15, s32[]{:T(128)S(6)} %add.38), kind=kOutput, calls=%fused_computation.6 | convolution fusion | flops 4831838208 | bytes 12058632 | tf_op jit(solution)/shard_map/tka,kn->tan/dot_general | solution.py:51
  99.1 53.9 %all-gather.3.cloned.1.call-done = f32[16,6,128,128]{3,2,1,0:T(8,128)} async-done(((f32[4,6,128,128]{3,2,1,0:T(8,128)}), f32[16,6,128,128]{3,2,1,0:T(8,128)}) %all-gather.3.cloned.1.call-update) | async-done | bytes 6291472 | tf_op jit(solution)/shard_map/all_gather | solution.py:46
  153.0 8.4 %add_bitcast_fusion = f32[16,16,4,8,128]{4,3,2,1,0:T(8,128)S(1)} fusion(f32[16,128,512]{2,1,0:T(8,128)} %fusion, f32[16,768,128]{2,1,0:T(8,128)} %bitcast.33, f32[2,1536,512]{2,1,0:T(8,128)} %constant_dynamic-update-slice_fusion, s32[]{:T(128)S(6)} %select_n.15), kind=kOutput, calls=%fused_computation.2 | convolution fusion | flops 4832886784 | bytes 16252932 | tf_op jit(solution)/shard_map/tka,kn->tan/dot_general | solution.py:51
  161.4 2.6 copy.31
  164.0 7.9 %fusion.1 = f32[16,128,512]{2,1,0:T(8,128)S(1)} fusion(f32[16,768,128]{2,1,0:T(8,128)} %bitcast.32, f32[2,1536,512]{2,1,0:T(8,128)} %constant_dynamic-update-slice_fusion, s32[]{:T(128)S(6)} %select_n.14, s32[]{:T(128)S(6)} %add.38), kind=kOutput, calls=%fused_computation.9 | convolution fusion | flops 4831838208 | bytes 12058632 | tf_op jit(solution)/shard_map/tka,kn->tan/dot_general | solution.py:51
  171.9 8.3 %convolution_add_fusion = f32[16,128,512]{2,1,0:T(8,128)} fusion(f32[16,128,512]{2,1,0:T(8,128)S(1)} %fusion.1, f32[16,768,128]{2,1,0:T(8,128)S(1)} %bitcast.36, f32[2,1536,512]{2,1,0:T(8,128)} %constant_dynamic-update-slice_fusion, s32[]{:T(128)S(6)} %select_n.14), kind=kOutput, calls=%fused_computation.4 | convolution fusion | flops 4832886784 | bytes 16252932 | tf_op jit(solution)/shard_map/tka,kn->tan/dot_general | solution.py:51
  180.2 5.2 %reshape.23 = f32[16,128,4,128]{3,2,1,0:T(4,128)} reshape(f32[16,128,512]{2,1,0:T(8,128)} %convolution_add_fusion) | data formatting | bytes 8388608 | tf_op jit(solution)/shard_map/reshape | solution.py:59
  185.4 6.4 %copy_add_fusion = f32[16,128,4,128]{3,1,2,0:T(8,128)} fusion(f32[16,128,4,128]{3,1,2,0:T(8,128)} %collective-permute-done.1, f32[16,128,4,128]{3,2,1,0:T(4,128)} %reshape.23), kind=kLoop, calls=%fused_computation.1 | loop fusion | flops 1048576 | bytes 12582912 | tf_op jit(solution)/shard_map/add | solution.py:60
  191.9 56.3 %reduce-scatter.2.cloned.1.call-done = f32[2,128,4,128]{3,1,2,0:T(8,128)} async-done(((f32[16,128,4,128]{3,1,2,0:T(8,128)}), f32[2,128,4,128]{3,1,2,0:T(8,128)}) %reduce-scatter.2.cloned.1.call-update) | async-done | bytes 524304 | tf_op jit(solution)/shard_map/reduce_scatter | solution.py:61
  248.2 1.1 constant_dynamic-slice_fusion
  249.3 1.9 collective-permute-start.2
  251.2 0.7 collective-permute-start.3
  251.9 7.1 %collective-permute-done.2 = f32[1,128,4,128]{3,1,2,0:T(8,128)S(1)} collective-permute-done((f32[1,128,4,128]{3,1,2,0:T(8,128)S(1)}, f32[1,128,4,128]{3,1,2,0:T(8,128)S(1)}, u32[]{:S(2)}, u32[]{:S(2)}) %collective-permute-start.2) | collective-permute-done | bytes 262176 | tf_op jit(solution)/shard_map/ppermute | solution.py:65
  259.1 0.9 copy.23
  (26 shorter events, 0.6 us)
Async XLA Ops:
  6.5 2.4 copy-start
  6.5 83.5 %all-gather.5.cloned.1.call-start = ((), (), s32[]{:S(2)}) async-start(), calls=%async_computation.2 | async-start | bytes 7864320 | tf_op jit(solution)/shard_map/all_gather | solution.py:46
  9.2 2.8 %copy-start.1 = (s32[12,4]{0,1:T(4,128)S(1)}, s32[12,4]{0,1:T(4,128)}, u32[]{:S(2)}) copy-start(s32[12,4]{0,1:T(4,128)} %param.8) | copy-start | bytes 580
  11.2 141.8 %all-gather.3.cloned.1.call-start = ((), (), s32[]{:S(2)}) async-start(), calls=%async_computation.1 | async-start | bytes 7864320 | tf_op jit(solution)/shard_map/all_gather | solution.py:46
  11.9 236.3 %reduce-scatter.2.cloned.1.call-start = ((), (), s32[]{:S(2)}) async-start(), calls=%async_computation.3 | async-start | bytes 4718592 | tf_op jit(solution)/shard_map/reduce_scatter | solution.py:61
  14.7 70.0 %collective-permute-start = (f32[12,128,4,128]{3,2,1,0:T(4,128)S(1)}, f32[12,128,4,128]{3,2,1,0:T(4,128)}, u32[]{:S(2)}, u32[]{:S(2)}) collective-permute-start(f32[12,128,4,128]{3,2,1,0:T(4,128)S(1)} %broadcast_multiply_fusion), channel_id=1, source_target_pairs={{0,4},{4,0},{1,5},{5,1},{2,6},{6,2},{3,7},{7,3},{8,12},{12,8},{9,1... | collective-permute-start | bytes 9437192 | tf_op jit(solution)/shard_map/ppermute | solution.py:34
  164.0 21.4 %collective-permute-start.1 = (f32[16,128,4,128]{3,1,2,0:T(8,128)}, f32[16,128,4,128]{3,1,2,0:T(8,128)}, u32[]{:S(2)}, u32[]{:S(2)}) collective-permute-start(f32[16,128,4,128]{3,1,2,0:T(8,128)} %bitcast.30), channel_id=1, source_target_pairs={{0,8},{8,0},{1,9},{9,1},{2,10},{10,2},{3,11},{11,3},{4,12},{12,4},... | collective-permute-start | bytes 12582920 | tf_op jit(solution)/shard_map/ppermute | solution.py:58
  164.0 7.9 %slice-start = ((s8[6291456]{0:T(1024)(128)(4,1)}), s8[2097152]{0:T(1024)(128)(4,1)S(1)}, s32[]{:S(2)}) async-start(s8[6291456]{0:T(1024)(128)(4,1)} %bitcast.34), calls=%async_computation.4 | async-start | bytes 4194304
  164.0 7.9 %slice-start.1 = ((s8[6291456]{0:T(1024)(128)(4,1)}), s8[4194304]{0:T(1024)(128)(4,1)S(1)}, s32[]{:S(2)}) async-start(s8[6291456]{0:T(1024)(128)(4,1)} %bitcast.34), calls=%async_computation.5 | async-start | bytes 8388608
  191.9 60.0 %copy-start.2 = (s32[1,4]{1,0:T(1,128)S(1)}, s32[1,4]{1,0:T(1,128)}, u32[]{:S(2)}) copy-start(s32[1,4]{1,0:T(1,128)} %param.9) | copy-start | bytes 52
  249.3 9.8 %collective-permute-start.2 = (f32[1,128,4,128]{3,1,2,0:T(8,128)S(1)}, f32[1,128,4,128]{3,1,2,0:T(8,128)S(1)}, u32[]{:S(2)}, u32[]{:S(2)}) collective-permute-start(f32[1,128,4,128]{3,1,2,0:T(8,128)S(1)} %get-tuple-element.8), channel_id=1, source_target_pairs={{0,0},{1,1},{2,2},{3,3},{4,132},{5,133},{6,134},{7,135},{8,4},{9,5... | collective-permute-start | bytes 786440 | tf_op jit(solution)/shard_map/ppermute | solution.py:65
  251.2 7.8 %collective-permute-start.3 = (f32[1,128,4,128]{3,1,2,0:T(8,128)S(1)}, f32[1,128,4,128]{3,1,2,0:T(8,128)S(1)}, u32[]{:S(2)}, u32[]{:S(2)}) collective-permute-start(f32[1,128,4,128]{3,1,2,0:T(8,128)S(1)} %get-tuple-element.7), channel_id=1, source_target_pairs={{0,8},{1,9},{2,10},{3,11},{4,140},{5,141},{6,142},{7,143},{8,12},{... | collective-permute-start | bytes 786440 | tf_op jit(solution)/shard_map/ppermute | solution.py:65
Sparse Core Ops, SparseCore 0:
  11.3 70.9 all-gather.4
  84.1 68.8 all-gather.2
  192.0 56.1 reduce-scatter.1

commit v5 on v4

--- a/solution.py
+++ b/solution.py
@@ -5,7 +5,6 @@
 from jax.sharding import PartitionSpec as P
 
 AXES = ("yhi", "z", "core", "ylo", "x")
-K_CHUNKS = 2
 
 
 def owner_perm(yhis, zs, cores, ylos, xs, flip):
@@ -13,13 +12,15 @@
         return (((yhi * zs + z) * cores + c) * ylos + ylo) * xs + x
 
     half = yhis * zs * cores // ylos
+    rows_per = half // xs
     pairs = []
     for yhi in range(yhis):
         for z in range(zs):
             for c in range(cores):
                 for ylo in range(ylos):
                     for x in range(xs):
-                        t = yhis * z + (yhi ^ flip)
+                        r = yhis * z + (yhi ^ flip)
+                        t = rows_per * ((x + r // rows_per) % xs) + r % rows_per
                         dst_blk = half * ylo + t
                         dyhi, rest = divmod(dst_blk, zs * cores)
                         dz, dc = divmod(rest, cores)
@@ -40,20 +41,18 @@
     keep_b = lax.dynamic_index_in_dim(both_b, core, 0, keepdims=False)
     send_b = lax.dynamic_index_in_dim(both_b, 1 - core, 0, keepdims=False)
 
-    step = masked_a.shape[2] // K_CHUNKS
-    send_part = keep_part = None
-    for c in range(K_CHUNKS):
-        rows_a = lax.all_gather(local_a[:, c * step:(c + 1) * step], "x", axis=0, tiled=True)
-        flat_a = rows_a.reshape(rows_a.shape[0], step * rows_a.shape[2], rows_a.shape[3])
-        lo, hi = c * step * side, (c + 1) * step * side
+    rows_a = lax.all_gather(local_a, "x", axis=0)
+    xs = rows_a.shape[0]
+    x = lax.axis_index("x")
+    pieces = [local_a] + [lax.dynamic_index_in_dim(rows_a, (x + d) % xs, 0, keepdims=False) for d in range(1, xs)]
 
-        def product(src):
-            return jnp.einsum("tka,kn->tan", flat_a, src[lo:hi], precision=lax.Precision.HIGH,
-                              preferred_element_type=jnp.float32)
+    def product(piece, src):
+        flat = piece.reshape(piece.shape[0], depth, piece.shape[3])
+        return jnp.einsum("tka,kn->tan", flat, src, precision=lax.Precision.HIGH,
+                          preferred_element_type=jnp.float32)
 
-        s, k = product(send_b), product(keep_b)
-        send_part = s if send_part is None else send_part + s
-        keep_part = k if keep_part is None else keep_part + k
+    send_part = jnp.concatenate([product(p, send_b) for p in pieces], axis=0)
+    keep_part = jnp.concatenate([product(p, keep_b) for p in pieces], axis=0)
     shape = (send_part.shape[0], send_part.shape[1], masked_b.shape[2], side)
     sent = lax.ppermute(send_part.reshape(shape), "core", [(0, 1), (1, 0)])
     (kept,) = lax.optimization_barrier((keep_part.reshape(shape),))

time: 270 us -> 281 us (1.041)
  the two profiles are of different devices: /device:TPU:24 before, /device:TPU:4 now
where the time goes in v5:
time: 281 us
  waiting for transfers between devices  175 us (62%)
  local copies, waits for them, and re-layouts  30.8 us (11%)
  matrix products  29.5 us (10%)
  other arithmetic  20 us (7%)
  between operations  13.7 us (5%)
  starting transfers between devices  12 us (4%)
    ppermute x1, waiting for transfers between devices, shards(): other_b = lax.ppermute(masked_b, 'ylo', [(0, 1), (1, 0)])  57.6 us
    reduce_scatter x1, waiting for transfers between devices, shards(): summed = lax.psum_scatter(summed, 'z', scatter_dimension=0, tiled=True)  56.9 us
    all_gather x1, waiting for transfers between devices, shards(): rows_a = lax.all_gather(local_a, 'x', axis=0)  37.2 us
    dot_general x8, matrix products, product(): jnp.einsum('tka,kn->tan', flat, src, precision=lax.Precision.HIGH, prefer...  29.5 us
    ppermute x1, waiting for transfers between devices, shards(): lax.ppermute(second, AXES, perms[1])  14.8 us
    another operation x3, local copies, waits for them, and re-layouts, shards(): jnp.stack([masked_b.reshape(depth, width), other_b.reshape(depth, width)])  10.6 us
    unnamed x30, local copies, waits for them, and re-layouts  8.22 us
    ppermute x1, waiting for transfers between devices, shards(): lax.ppermute(first, AXES, perms[0]) + lax.ppermute(second, AXES, perms[1])  8.02 us
  transfers between devices with their start and end apart: 6, of which 5 were waited for; matrix products, arithmetic and copies ran while one was open for 18% of the time, Pallas kernels for 0%

profile of v5, /device:TPU:4, one launch (start us, length us, event | category | flops | bytes accessed | tf_op | source)
XLA Modules:
  0.0 280.5 jit_solution(12530265347335427272)
XLA Ops:
  11.7 4.3 %broadcast_multiply_fusion = f32[12,128,4,128]{3,2,1,0:T(4,128)} fusion(f32[12,128,4,128]{3,2,1,0:T(4,128)} %param.7, f32[12,4]{1,0:T(8,128)S(1)} %copy.21), kind=kLoop, calls=%fused_computation.28 | loop fusion | flops 786432 | bytes 6291648 | tf_op jit(solution)/shard_map/mul | solution.py:33
  17.6 5.2 %stack_reshape.6 = f32[1,1536,512]{2,1,0:T(8,128)} reshape(f32[12,128,4,128]{3,2,1,0:T(4,128)} %broadcast_multiply_fusion) | data formatting | bytes 6291456 | tf_op jit(solution)/shard_map/stack;reshape | solution.py:39
  22.8 3.8 %constant_dynamic-update-slice_fusion.1 = f32[2,1536,512]{2,1,0:T(8,128)} fusion(f32[1,1536,512]{2,1,0:T(8,128)} %stack_reshape.6), kind=kLoop, calls=%fused_computation.32 | loop fusion | bytes 6291456
  28.6 57.6 %collective-permute-done = f32[12,128,4,128]{3,2,1,0:T(4,128)} collective-permute-done((f32[12,128,4,128]{3,2,1,0:T(4,128)}, f32[12,128,4,128]{3,2,1,0:T(4,128)}, u32[]{:S(2)}, u32[]{:S(2)}) %collective-permute-start) | collective-permute-done | bytes 3145760 | tf_op jit(solution)/shard_map/ppermute | solution.py:35
  86.2 3.5 %stack_reshape.7 = f32[1,1536,512]{2,1,0:T(8,128)S(1)} reshape(f32[12,128,4,128]{3,2,1,0:T(4,128)} %collective-permute-done) | data formatting | bytes 6291456 | tf_op jit(solution)/shard_map/stack;reshape | solution.py:39
  92.7 4.9 %fusion.6 = f32[4,128,512]{2,1,0:T(8,128)S(1)} fusion(f32[4,1536,128]{2,1,0:T(8,128)S(1)} %bitcast.48, f32[2,1536,512]{2,1,0:T(8,128)} %constant_dynamic-update-slice_fusion, s32[]{:T(128)S(6)} %select_n.46), kind=kOutput, calls=%fused_computation.10 | convolution fusion | flops 2415919104 | bytes 7340036 | tf_op jit(solution)/shard_map/tka,kn->tan/dot_general | solution.py:51
  97.6 37.2 %all-gather.3.cloned.1.call-done = f32[16,12,128,128]{3,2,1,0:T(8,128)} async-done(((f32[4,12,128,128]{3,2,1,0:T(8,128)}), f32[16,12,128,128]{3,2,1,0:T(8,128)}) %all-gather.3.cloned.1.call-update) | async-done | bytes 12582928 | tf_op jit(solution)/shard_map/all_gather | solution.py:44
  134.8 4.6 %constant_dynamic-slice_fusion.4 = (f32[1,4,12,128,128]{4,3,2,1,0:T(8,128)S(1)}, f32[1,4,12,128,128]{4,3,2,1,0:T(8,128)S(1)}, f32[1,4,12,128,128]{4,3,2,1,0:T(8,128)S(1)}) fusion(f32[4,4,12,128,128]{4,3,2,1,0:T(8,128)} %bitcast.55, s32[]{:T(128)S(6)} %select_n.41, s32[]{:T(128)S(6)} %select_n.45, s32[]{:T(128)S(6)} %select_n.43), kind=kLoop, calls=%fused_computation.44 | loop fusion | bytes 18874380 | tf_op jit(solution)/shard_map/jit(dynamic_index_in_dim)/dynamic_slice | solution.py:47
  139.8 2.8 fusion
  142.6 2.8 fusion.2
  145.3 3.0 %fusion.4 = f32[4,128,512]{2,1,0:T(8,128)S(1)} fusion(f32[4,1536,128]{2,1,0:T(8,128)S(1)} %bitcast.49, f32[2,1536,512]{2,1,0:T(8,128)S(1)} %bitcast.44, s32[]{:T(128)S(6)} %select_n.46), kind=kOutput, calls=%fused_computation.8 | convolution fusion | flops 2415919104 | bytes 7340036 | tf_op jit(solution)/shard_map/tka,kn->tan/dot_general | solution.py:51
  148.4 2.6 copy_bitcast_fusion
  151.0 5.6 %fusion.14 = f32[4,128,512]{2,1,0:T(8,128)S(1)} fusion(f32[4,1536,128]{2,1,0:T(8,128)} %bitcast.47, f32[2,1536,512]{2,1,0:T(8,128)} %constant_dynamic-update-slice_fusion, s32[]{:T(128)S(6)} %select_n.39), kind=kOutput, calls=%fused_computation.18 | convolution fusion | flops 2415919104 | bytes 7340036 | tf_op jit(solution)/shard_map/tka,kn->tan/dot_general | solution.py:51
  156.6 4.8 %fusion.8 = f32[4,128,512]{2,1,0:T(8,128)S(1)} fusion(f32[4,1536,128]{2,1,0:T(8,128)S(1)} %bitcast.54, f32[2,1536,512]{2,1,0:T(8,128)} %constant_dynamic-update-slice_fusion, s32[]{:T(128)S(6)} %select_n.39), kind=kOutput, calls=%fused_computation.12 | convolution fusion | flops 2415919104 | bytes 7340036 | tf_op jit(solution)/shard_map/tka,kn->tan/dot_general | solution.py:51
  161.5 2.8 %fusion.10 = f32[4,128,512]{2,1,0:T(8,128)S(1)} fusion(f32[4,1536,128]{2,1,0:T(8,128)S(1)} %bitcast.52, f32[2,1536,512]{2,1,0:T(8,128)S(1)} %bitcast.46, s32[]{:T(128)S(6)} %select_n.39), kind=kOutput, calls=%fused_computation.14 | convolution fusion | flops 2415919104 | bytes 7340036 | tf_op jit(solution)/shard_map/tka,kn->tan/dot_general | solution.py:51
  164.3 2.8 %fusion.12 = f32[4,128,512]{2,1,0:T(8,128)S(1)} fusion(f32[4,1536,128]{2,1,0:T(8,128)S(1)} %bitcast.50, f32[2,1536,512]{2,1,0:T(8,128)S(1)} %bitcast.46, s32[]{:T(128)S(6)} %select_n.39), kind=kOutput, calls=%fused_computation.16 | convolution fusion | flops 2415919104 | bytes 7340036 | tf_op jit(solution)/shard_map/tka,kn->tan/dot_general | solution.py:51
  167.2 2.6 pad_maximum_fusion
  169.7 5.3 %reshape.34 = f32[16,128,4,128]{3,2,1,0:T(4,128)} reshape(f32[16,128,512]{2,1,0:T(8,128)} %pad_maximum_fusion) | data formatting | bytes 8388608 | tf_op jit(solution)/shard_map/reshape | solution.py:58
  175.0 6.5 %copy_add_fusion = f32[16,128,4,128]{3,1,2,0:T(8,128)} fusion(f32[16,128,4,128]{3,1,2,0:T(8,128)} %collective-permute-done.1, f32[16,128,4,128]{3,2,1,0:T(4,128)} %reshape.34), kind=kLoop, calls=%fused_computation.3 | loop fusion | flops 1048576 | bytes 12582912 | tf_op jit(solution)/shard_map/add | solution.py:59
  181.5 56.9 %reduce-scatter.2.cloned.1.call-done = f32[2,128,4,128]{3,1,2,0:T(8,128)} async-done(((f32[16,128,4,128]{3,1,2,0:T(8,128)}), f32[2,128,4,128]{3,1,2,0:T(8,128)}) %reduce-scatter.2.cloned.1.call-update) | async-done | bytes 524304 | tf_op jit(solution)/shard_map/reduce_scatter | solution.py:60
  239.5 5.0 %collective-permute-start.2 = (f32[1,128,4,128]{3,1,2,0:T(8,128)S(1)}, f32[1,128,4,128]{3,1,2,0:T(8,128)S(1)}, u32[]{:S(2)}, u32[]{:S(2)}) collective-permute-start(f32[1,128,4,128]{3,1,2,0:T(8,128)S(1)} %get-tuple-element.9), channel_id=1, source_target_pairs={{0,0},{1,33},{2,66},{3,99},{4,132},{5,165},{6,198},{7,231},{8,4},{... | collective-permute-start | bytes 786440 | tf_op jit(solution)/shard_map/ppermute | solution.py:64
  244.5 5.4 %collective-permute-start.3 = (f32[1,128,4,128]{3,1,2,0:T(8,128)S(1)}, f32[1,128,4,128]{3,1,2,0:T(8,128)S(1)}, u32[]{:S(2)}, u32[]{:S(2)}) collective-permute-start(f32[1,128,4,128]{3,1,2,0:T(8,128)S(1)} %get-tuple-element.8), channel_id=1, source_target_pairs={{0,8},{1,41},{2,74},{3,107},{4,140},{5,173},{6,206},{7,239},{8,12}... | collective-permute-start | bytes 786440 | tf_op jit(solution)/shard_map/ppermute | solution.py:64
  249.9 8.0 %collective-permute-done.2 = f32[1,128,4,128]{3,1,2,0:T(8,128)S(1)} collective-permute-done((f32[1,128,4,128]{3,1,2,0:T(8,128)S(1)}, f32[1,128,4,128]{3,1,2,0:T(8,128)S(1)}, u32[]{:S(2)}, u32[]{:S(2)}) %collective-permute-start.2) | collective-permute-done | bytes 262176 | tf_op jit(solution)/shard_map/ppermute | solution.py:64
  257.9 14.8 %collective-permute-done.3 = f32[1,128,4,128]{3,1,2,0:T(8,128)S(1)} collective-permute-done((f32[1,128,4,128]{3,1,2,0:T(8,128)S(1)}, f32[1,128,4,128]{3,1,2,0:T(8,128)S(1)}, u32[]{:S(2)}, u32[]{:S(2)}) %collective-permute-start.3) | collective-permute-done | bytes 262176 | tf_op jit(solution)/shard_map/ppermute | solution.py:64
  (48 shorter events, 14.1 us)
Async XLA Ops:
  6.5 2.4 copy-start.7
  6.5 128.3 %all-gather.3.cloned.1.call-start = ((), (), s32[]{:S(2)}) async-start(), calls=%async_computation.2 | async-start | bytes 15728640 | tf_op jit(solution)/shard_map/all_gather | solution.py:44
  10.9 0.7 copy-start.8
  11.0 227.5 %reduce-scatter.2.cloned.1.call-start = ((), (), s32[]{:S(2)}) async-start(), calls=%async_computation.1 | async-start | bytes 4718592 | tf_op jit(solution)/shard_map/reduce_scatter | solution.py:60
  16.0 70.2 %collective-permute-start = (f32[12,128,4,128]{3,2,1,0:T(4,128)}, f32[12,128,4,128]{3,2,1,0:T(4,128)}, u32[]{:S(2)}, u32[]{:S(2)}) collective-permute-start(f32[12,128,4,128]{3,2,1,0:T(4,128)} %broadcast_multiply_fusion), channel_id=1, source_target_pairs={{0,4},{4,0},{1,5},{5,1},{2,6},{6,2},{3,7},{7,3},{8,12},{12,8},{9,1... | collective-permute-start | bytes 9437192 | tf_op jit(solution)/shard_map/ppermute | solution.py:35
  89.7 3.0 %copy-start = (f32[4,128,12,128]{1,3,2,0:T(8,128)S(1)}, f32[4,128,12,128]{1,3,2,0:T(8,128)}, u32[]{:S(2)}) copy-start(f32[4,128,12,128]{1,3,2,0:T(8,128)} %broadcast_multiply_fusion.1) | copy-start | bytes 9437188
  92.7 46.8 %slice-start = ((s8[6291456]{0:T(1024)(128)(4,1)}), s8[2097152]{0:T(1024)(128)(4,1)S(1)}, s32[]{:S(2)}) async-start(s8[6291456]{0:T(1024)(128)(4,1)} %bitcast.43), calls=%async_computation.3 | async-start | bytes 4194304
  134.8 4.9 %slice-start.1 = ((s8[6291456]{0:T(1024)(128)(4,1)}), s8[4194304]{0:T(1024)(128)(4,1)S(1)}, s32[]{:S(2)}) async-start(s8[6291456]{0:T(1024)(128)(4,1)} %bitcast.43), calls=%async_computation.4 | async-start | bytes 8388608
  139.5 3.1 %copy-start.3 = (f32[1,4,12,128,128]{4,3,2,1,0:T(8,128)}, f32[1,4,12,128,128]{4,3,2,1,0:T(8,128)S(1)}, u32[]{:S(2)}) copy-start(f32[1,4,12,128,128]{4,3,2,1,0:T(8,128)S(1)} %get-tuple-element.7) | copy-start | bytes 9437188
  139.5 5.9 %copy-start.1 = (f32[1,4,12,128,128]{4,3,2,1,0:T(8,128)}, f32[1,4,12,128,128]{4,3,2,1,0:T(8,128)S(1)}, u32[]{:S(2)}) copy-start(f32[1,4,12,128,128]{4,3,2,1,0:T(8,128)S(1)} %get-tuple-element.5) | copy-start | bytes 9437188
  139.5 8.9 %copy-start.5 = (f32[1,4,12,128,128]{4,3,2,1,0:T(8,128)}, f32[1,4,12,128,128]{4,3,2,1,0:T(8,128)S(1)}, u32[]{:S(2)}) copy-start(f32[1,4,12,128,128]{4,3,2,1,0:T(8,128)S(1)} %get-tuple-element.6) | copy-start | bytes 9437188
  148.4 13.1 %slice-start.2 = ((s8[6291456]{0:T(1024)(128)(4,1)}), s8[2097152]{0:T(1024)(128)(4,1)S(1)}, s32[]{:S(2)}) async-start(s8[6291456]{0:T(1024)(128)(4,1)} %bitcast.45), calls=%async_computation.5 | async-start | bytes 4194304
  151.0 24.0 %collective-permute-start.1 = (f32[16,128,4,128]{3,1,2,0:T(8,128)}, f32[16,128,4,128]{3,1,2,0:T(8,128)}, u32[]{:S(2)}, u32[]{:S(2)}) collective-permute-start(f32[16,128,4,128]{3,1,2,0:T(8,128)} %copy_bitcast_fusion), channel_id=1, source_target_pairs={{0,8},{8,0},{1,9},{9,1},{2,10},{10,2},{3,11},{11,3},{4,12},{12,4},... | collective-permute-start | bytes 12582920 | tf_op jit(solution)/shard_map/ppermute | solution.py:57
  151.0 5.6 %copy-start.6 = (f32[1,4,12,128,128]{4,3,2,1,0:T(8,128)S(1)}, f32[1,4,12,128,128]{4,3,2,1,0:T(8,128)}, u32[]{:S(2)}) copy-start(f32[1,4,12,128,128]{4,3,2,1,0:T(8,128)} %copy-done.5) | copy-start | bytes 9437188
  151.0 10.5 %slice-start.3 = ((s8[6291456]{0:T(1024)(128)(4,1)}), s8[4194304]{0:T(1024)(128)(4,1)S(1)}, s32[]{:S(2)}) async-start(s8[6291456]{0:T(1024)(128)(4,1)} %bitcast.45), calls=%async_computation.6 | async-start | bytes 8388608
  156.6 4.8 %copy-start.4 = (f32[1,4,12,128,128]{4,3,2,1,0:T(8,128)S(1)}, f32[1,4,12,128,128]{4,3,2,1,0:T(8,128)}, u32[]{:S(2)}) copy-start(f32[1,4,12,128,128]{4,3,2,1,0:T(8,128)} %copy-done.3) | copy-start | bytes 9437188
  161.5 2.8 %copy-start.2 = (f32[1,4,12,128,128]{4,3,2,1,0:T(8,128)S(1)}, f32[1,4,12,128,128]{4,3,2,1,0:T(8,128)}, u32[]{:S(2)}) copy-start(f32[1,4,12,128,128]{4,3,2,1,0:T(8,128)} %copy-done.1) | copy-start | bytes 9437188
  181.5 68.4 %copy-start.9 = (s32[1,4]{1,0:T(1,128)S(1)}, s32[1,4]{1,0:T(1,128)}, u32[]{:S(2)}) copy-start(s32[1,4]{1,0:T(1,128)} %param.9) | copy-start | bytes 52
  239.5 18.4 %collective-permute-start.2 = (f32[1,128,4,128]{3,1,2,0:T(8,128)S(1)}, f32[1,128,4,128]{3,1,2,0:T(8,128)S(1)}, u32[]{:S(2)}, u32[]{:S(2)}) collective-permute-start(f32[1,128,4,128]{3,1,2,0:T(8,128)S(1)} %get-tuple-element.9), channel_id=1, source_target_pairs={{0,0},{1,33},{2,66},{3,99},{4,132},{5,165},{6,198},{7,231},{8,4},{... | collective-permute-start | bytes 786440 | tf_op jit(solution)/shard_map/ppermute | solution.py:64
  244.5 28.3 %collective-permute-start.3 = (f32[1,128,4,128]{3,1,2,0:T(8,128)S(1)}, f32[1,128,4,128]{3,1,2,0:T(8,128)S(1)}, u32[]{:S(2)}, u32[]{:S(2)}) collective-permute-start(f32[1,128,4,128]{3,1,2,0:T(8,128)S(1)} %get-tuple-element.8), channel_id=1, source_target_pairs={{0,8},{1,41},{2,74},{3,107},{4,140},{5,173},{6,206},{7,239},{8,12}... | collective-permute-start | bytes 786440 | tf_op jit(solution)/shard_map/ppermute | solution.py:64
Sparse Core Ops, SparseCore 0:
  11.1 123.7 all-gather.2
  181.6 56.7 reduce-scatter.1

commit v6 on v4

--- a/solution.py
+++ b/solution.py
@@ -48,15 +48,15 @@
         lo, hi = c * step * side, (c + 1) * step * side
 
         def product(src):
-            return jnp.einsum("tka,kn->tan", flat_a, src[lo:hi], precision=lax.Precision.HIGH,
+            blocks = src[lo:hi].reshape(hi - lo, masked_b.shape[2], side)
+            return jnp.einsum("tka,kcd->tacd", flat_a, blocks, precision=lax.Precision.HIGH,
                               preferred_element_type=jnp.float32)
 
         s, k = product(send_b), product(keep_b)
         send_part = s if send_part is None else send_part + s
         keep_part = k if keep_part is None else keep_part + k
-    shape = (send_part.shape[0], send_part.shape[1], masked_b.shape[2], side)
-    sent = lax.ppermute(send_part.reshape(shape), "core", [(0, 1), (1, 0)])
-    (kept,) = lax.optimization_barrier((keep_part.reshape(shape),))
+    sent = lax.ppermute(send_part, "core", [(0, 1), (1, 0)])
+    (kept,) = lax.optimization_barrier((keep_part,))
     summed = kept + sent
     summed = lax.psum_scatter(summed, "z", scatter_dimension=0, tiled=True)
     yhi = lax.axis_index("yhi")

time: 270 us -> 276 us (1.022)
  matrix products: 33.6 us -> 51.1 us
  waiting for transfers between devices: 181 us -> 164 us
  local copies, waits for them, and re-layouts: 26.2 us -> 33.5 us
    dot_general x4, matrix products: 33.6 us -> 51.1 us  [product(): jnp.einsum('tka,kcd->tacd', flat_a, blocks, precision=lax.Precision.HIGH,...]
    all_gather x2, waiting for transfers between devices: 53.9 us -> 37.3 us  [shards(): lax.all_gather(local_a[:, c * step:(c + 1) * step], 'x', axis=0, tiled=True)]
    slice x0 -> x5, local copies, waits for them, and re-layouts: none -> 15.2 us  [product(): blocks = src[lo:hi].reshape(hi - lo, masked_b.shape[2], side)]
    reshape x2 -> x0, local copies, waits for them, and re-layouts: 7.86 us -> none  [the longest x1 5.25 us: shards(): kept, = lax.optimization_barrier((keep_part.reshape(shape),))]
    unnamed x12 -> x16, local copies, waits for them, and re-layouts: 6.25 us -> 6.24 us
  transfers between devices with their start and end apart: 7 -> 7, of which waited for: 4 -> 4; matrix products, arithmetic and copies ran while one was open for 17% -> 24% of each run, Pallas kernels for 0% -> 0%
where the time goes in v6:
time: 276 us; the launch traced here: 273 us
  waiting for transfers between devices  164 us (59%)
  matrix products  51.1 us (19%)
  local copies, waits for them, and re-layouts  33.5 us (12%)
  between operations  13.3 us (5%)
  other arithmetic  7.99 us (3%)
  starting transfers between devices  3.51 us (1%)
    ppermute x1, waiting for transfers between devices, shards(): other_b = lax.ppermute(masked_b, 'ylo', [(0, 1), (1, 0)])  62.5 us
    reduce_scatter x1, waiting for transfers between devices, shards(): summed = lax.psum_scatter(summed, 'z', scatter_dimension=0, tiled=True)  56.3 us
    dot_general x4, matrix products, product(): jnp.einsum('tka,kcd->tacd', flat_a, blocks, precision=lax.Precision.HIGH,...  51.1 us
    all_gather x2, waiting for transfers between devices, shards(): lax.all_gather(local_a[:, c * step:(c + 1) * step], 'x', axis=0, tiled=True)  37.3 us
    slice x5, local copies, waits for them, and re-layouts, product(): blocks = src[lo:hi].reshape(hi - lo, masked_b.shape[2], side)  15.2 us
    another operation x3, local copies, waits for them, and re-layouts, shards(): jnp.stack([masked_b.reshape(depth, width), other_b.reshape(depth, width)])  8.15 us
    ppermute x1, waiting for transfers between devices, shards(): lax.ppermute(first, AXES, perms[0]) + lax.ppermute(second, AXES, perms[1])  7.14 us
    unnamed x16, local copies, waits for them, and re-layouts  6.24 us
  transfers between devices with their start and end apart: 7, of which 4 were waited for; matrix products, arithmetic and copies ran while one was open for 24% of the time, Pallas kernels for 0%

profile of v6, /device:TPU:24, one launch (start us, length us, event | category | flops | bytes accessed | tf_op | source)
XLA Modules:
  0.0 273.3 jit_solution(5139379151668989142)
XLA Ops:
  6.5 2.4 copy.38
  9.2 1.9 fusion
  12.1 2.6 broadcast_multiply_fusion
  15.5 2.9 %stack_reshape.6 = f32[1,1536,512]{2,1,0:T(8,128)} reshape(f32[12,128,4,128]{3,2,1,0:T(4,128)S(1)} %broadcast_multiply_fusion) | data formatting | bytes 6291456 | tf_op jit(solution)/shard_map/stack;reshape | solution.py:38
  18.4 3.8 %constant_dynamic-update-slice_fusion.1 = f32[2,1536,512]{2,1,0:T(8,128)} fusion(f32[1,1536,512]{2,1,0:T(8,128)} %stack_reshape.6), kind=kLoop, calls=%fused_computation.6 | loop fusion | bytes 6291456
  22.2 62.5 %collective-permute-done = f32[12,128,4,128]{3,2,1,0:T(4,128)} collective-permute-done((f32[12,128,4,128]{3,2,1,0:T(4,128)S(1)}, f32[12,128,4,128]{3,2,1,0:T(4,128)}, u32[]{:S(2)}, u32[]{:S(2)}) %collective-permute-start) | collective-permute-done | bytes 3145760 | tf_op jit(solution)/shard_map/ppermute | solution.py:34
  84.7 3.3 %stack_reshape.7 = f32[1,1536,512]{2,1,0:T(8,128)S(1)} reshape(f32[12,128,4,128]{3,2,1,0:T(4,128)} %collective-permute-done) | data formatting | bytes 6291456 | tf_op jit(solution)/shard_map/stack;reshape | solution.py:38
  88.0 2.0 constant_dynamic-update-slice_fusion
  90.0 5.6 %constant_dynamic-slice_fusion.4 = (f32[1,768,512]{2,1,0:T(8,128)}, f32[1,768,512]{2,1,0:T(8,128)}, f32[1,768,512]{2,1,0:T(8,128)S(1)}, f32[1,768,512]{2,1,0:T(8,128)S(1)}) fusion(f32[2,1536,512]{2,1,0:T(8,128)} %constant_dynamic-update-slice_fusion, s32[]{:T(128)S(6)} %select_n.15, s32[]{:T(128)S(6)} %add.38, s32[]{:T(128)S(6)} %select_n.14), kind=kLoop, calls=%fused_computation.11 | loop fusion | bytes 12582924 | tf_op jit(solution)/shard_map/slice | solution.py:51
  95.6 3.2 %copy.46 = f32[1,768,512]{1,2,0:T(8,128)} copy(f32[1,768,512]{2,1,0:T(8,128)} %get-tuple-element.6) | data formatting | bytes 3145728 | tf_op jit(solution)/shard_map/slice | solution.py:51
  98.8 3.1 %copy.49 = f32[1,768,512]{1,2,0:T(8,128)} copy(f32[1,768,512]{2,1,0:T(8,128)} %get-tuple-element.5) | data formatting | bytes 3145728 | tf_op jit(solution)/shard_map/slice | solution.py:51
  101.9 13.8 %fusion.2 = f32[16,128,4,128]{3,1,2,0:T(8,128)} fusion(f32[16,768,128,1]{2,1,3,0:T(8,128)} %bitcast.36, f32[768,4,128,1]{0,2,1,3:T(8,128)} %bitcast.42), kind=kOutput, calls=%fused_computation.16 | convolution fusion | flops 4831838208 | bytes 12058624 | tf_op jit(solution)/shard_map/tka,kcd->tacd/dot_general | solution.py:52
  115.7 37.3 %all-gather.5.cloned.1.call-done = f32[16,6,128,128]{3,2,1,0:T(8,128)} async-done(((f32[4,6,128,128]{3,2,1,0:T(8,128)}), f32[16,6,128,128]{3,2,1,0:T(8,128)}) %all-gather.5.cloned.1.call-update) | async-done | bytes 6291472 | tf_op jit(solution)/shard_map/all_gather | solution.py:46
  152.9 14.4 %convolution_add_fusion = f32[16,128,4,128]{3,1,2,0:T(8,128)} fusion(f32[16,128,4,128]{3,1,2,0:T(8,128)} %fusion.2, f32[16,768,128,1]{2,1,3,0:T(8,128)} %bitcast.38, f32[768,4,128,1]{0,2,1,3:T(8,128)} %bitcast.44), kind=kOutput, calls=%fused_computation.1 | convolution fusion | flops 4832886784 | bytes 16252928 | tf_op jit(solution)/shard_map/tka,kcd->tacd/dot_general | solution.py:52
  167.3 1.7 copy.40
  169.0 1.7 copy.43
  170.7 12.4 %fusion.1 = f32[16,128,4,128]{3,1,2,0:T(8,128)S(1)} fusion(f32[16,768,128,1]{2,1,3,0:T(8,128)} %bitcast.37, f32[768,4,128,1]{0,2,1,3:T(8,128)S(1)} %bitcast.43), kind=kOutput, calls=%fused_computation.15 | convolution fusion | flops 4831838208 | bytes 12058624 | tf_op jit(solution)/shard_map/tka,kcd->tacd/dot_general | solution.py:52
  183.1 10.5 %convolution_add_fusion.1 = f32[16,128,4,128]{3,1,2,0:T(8,128)S(1)} fusion(f32[16,128,4,128]{3,1,2,0:T(8,128)S(1)} %fusion.1, f32[16,768,128,1]{2,1,3,0:T(8,128)S(1)} %bitcast.41, f32[768,4,128,1]{0,2,1,3:T(8,128)S(1)} %bitcast.45), kind=kOutput, calls=%fused_computation.2 | convolution fusion | flops 4832886784 | bytes 16252928 | tf_op jit(solution)/shard_map/tka,kcd->tacd/dot_general | solution.py:52
  193.6 5.0 %add.34 = f32[16,128,4,128]{3,1,2,0:T(8,128)} add(f32[16,128,4,128]{3,1,2,0:T(8,128)S(1)} %convolution_add_fusion.1, f32[16,128,4,128]{3,1,2,0:T(8,128)} %collective-permute-done.1) | non-fusion elementwise | flops 1048576 | bytes 12582912 | tf_op jit(solution)/shard_map/add | solution.py:60
  198.7 56.3 %reduce-scatter.2.cloned.1.call-done = f32[2,128,4,128]{3,1,2,0:T(8,128)} async-done(((f32[16,128,4,128]{3,1,2,0:T(8,128)}), f32[2,128,4,128]{3,1,2,0:T(8,128)}) %reduce-scatter.2.cloned.1.call-update) | async-done | bytes 524304 | tf_op jit(solution)/shard_map/reduce_scatter | solution.py:61
  255.0 1.1 constant_dynamic-slice_fusion.2
  256.0 1.9 collective-permute-start.2
  258.7 7.1 %collective-permute-done.2 = f32[1,128,4,128]{3,1,2,0:T(8,128)S(1)} collective-permute-done((f32[1,128,4,128]{3,1,2,0:T(8,128)S(1)}, f32[1,128,4,128]{3,1,2,0:T(8,128)S(1)}, u32[]{:S(2)}, u32[]{:S(2)}) %collective-permute-start.2) | collective-permute-done | bytes 262176 | tf_op jit(solution)/shard_map/ppermute | solution.py:65
  265.9 0.9 copy.52
  (33 shorter events, 2.8 us)
Async XLA Ops:
  6.5 2.4 copy-start.2
  6.5 95.4 %all-gather.3.cloned.1.call-start = ((), (), s32[]{:S(2)}) async-start(), calls=%async_computation.1 | async-start | bytes 7864320 | tf_op jit(solution)/shard_map/all_gather | solution.py:46
  11.1 0.8 copy-start.3
  11.2 141.8 %all-gather.5.cloned.1.call-start = ((), (), s32[]{:S(2)}) async-start(), calls=%async_computation.2 | async-start | bytes 7864320 | tf_op jit(solution)/shard_map/all_gather | solution.py:46
  11.9 243.1 %reduce-scatter.2.cloned.1.call-start = ((), (), s32[]{:S(2)}) async-start(), calls=%async_computation.3 | async-start | bytes 4718592 | tf_op jit(solution)/shard_map/reduce_scatter | solution.py:61
  14.7 70.0 %collective-permute-start = (f32[12,128,4,128]{3,2,1,0:T(4,128)S(1)}, f32[12,128,4,128]{3,2,1,0:T(4,128)}, u32[]{:S(2)}, u32[]{:S(2)}) collective-permute-start(f32[12,128,4,128]{3,2,1,0:T(4,128)S(1)} %broadcast_multiply_fusion), channel_id=1, source_target_pairs={{0,4},{4,0},{1,5},{5,1},{2,6},{6,2},{3,7},{7,3},{8,12},{12,8},{9,1... | collective-permute-start | bytes 9437192 | tf_op jit(solution)/shard_map/ppermute | solution.py:34
  167.3 26.3 %collective-permute-start.1 = (f32[16,128,4,128]{3,1,2,0:T(8,128)}, f32[16,128,4,128]{3,1,2,0:T(8,128)}, u32[]{:S(2)}, u32[]{:S(2)}) collective-permute-start(f32[16,128,4,128]{3,1,2,0:T(8,128)} %convolution_add_fusion), channel_id=1, source_target_pairs={{0,8},{8,0},{1,9},{9,1},{2,10},{10,2},{3,11},{11,3},{4,12},{12,4},... | collective-permute-start | bytes 12582920 | tf_op jit(solution)/shard_map/ppermute | solution.py:58
  169.0 1.7 copy-start
  170.7 12.4 %slice-start = ((s8[6291456]{0:T(1024)(128)(4,1)}), s8[4194304]{0:T(1024)(128)(4,1)S(1)}, s32[]{:S(2)}) async-start(s8[6291456]{0:T(1024)(128)(4,1)} %bitcast.39), calls=%async_computation.4 | async-start | bytes 8388608
  170.7 12.4 %slice-start.1 = ((s8[6291456]{0:T(1024)(128)(4,1)}), s8[2097152]{0:T(1024)(128)(4,1)S(1)}, s32[]{:S(2)}) async-start(s8[6291456]{0:T(1024)(128)(4,1)} %bitcast.39), calls=%async_computation.5 | async-start | bytes 4194304
  170.7 12.4 %copy-start.1 = (f32[1,768,512]{1,2,0:T(8,128)S(1)}, f32[1,768,512]{1,2,0:T(8,128)}, u32[]{:S(2)}) copy-start(f32[1,768,512]{1,2,0:T(8,128)} %copy.43) | copy-start | bytes 4718596
  198.6 60.0 %copy-start.4 = (s32[1,4]{1,0:T(1,128)S(1)}, s32[1,4]{1,0:T(1,128)}, u32[]{:S(2)}) copy-start(s32[1,4]{1,0:T(1,128)} %param.9) | copy-start | bytes 52
  256.0 9.8 %collective-permute-start.2 = (f32[1,128,4,128]{3,1,2,0:T(8,128)S(1)}, f32[1,128,4,128]{3,1,2,0:T(8,128)S(1)}, u32[]{:S(2)}, u32[]{:S(2)}) collective-permute-start(f32[1,128,4,128]{3,1,2,0:T(8,128)S(1)} %get-tuple-element.12), channel_id=1, source_target_pairs={{0,0},{1,1},{2,2},{3,3},{4,132},{5,133},{6,134},{7,135},{8,4},{9,5... | collective-permute-start | bytes 786440 | tf_op jit(solution)/shard_map/ppermute | solution.py:65
  258.0 7.8 %collective-permute-start.3 = (f32[1,128,4,128]{3,1,2,0:T(8,128)S(1)}, f32[1,128,4,128]{3,1,2,0:T(8,128)S(1)}, u32[]{:S(2)}, u32[]{:S(2)}) collective-permute-start(f32[1,128,4,128]{3,1,2,0:T(8,128)S(1)} %get-tuple-element.11), channel_id=1, source_target_pairs={{0,8},{1,9},{2,10},{3,11},{4,140},{5,141},{6,142},{7,143},{8,12},{... | collective-permute-start | bytes 786440 | tf_op jit(solution)/shard_map/ppermute | solution.py:65
Sparse Core Ops, SparseCore 0:
  11.3 70.9 all-gather.2
  84.0 68.8 all-gather.4
  198.8 56.1 reduce-scatter.1

commit v7 on v4

--- a/solution.py
+++ b/solution.py
@@ -5,7 +5,7 @@
 from jax.sharding import PartitionSpec as P
 
 AXES = ("yhi", "z", "core", "ylo", "x")
-K_CHUNKS = 2
+K_CHUNKS = 1
 
 
 def owner_perm(yhis, zs, cores, ylos, xs, flip):

time: 270 us -> 269 us (level)
  waiting for transfers between devices: 181 us -> 163 us
  matrix products: 33.6 us -> 48.2 us
    all_gather x2 -> x1, waiting for transfers between devices: 53.9 us -> 36.4 us  [shards(): lax.all_gather(local_a[:, c * step:(c + 1) * step], 'x', axis=0, tiled=True)]
    dot_general x4 -> x2, matrix products: 33.6 us -> 48.2 us  [product(): jnp.einsum('tka,kn->tan', flat_a, src[lo:hi], precision=lax.Precision.HIG...]
    dynamic_slice x0 -> x3, local copies, waits for them, and re-layouts: none -> 11.2 us  [the longest x2 8.86 us: shards(): send_b = lax.dynamic_index_in_dim(both_b, 1 - core, 0, keepdims=False)]
    reshape x2 -> x0, local copies, waits for them, and re-layouts: 7.86 us -> none  [the longest x1 5.25 us: shards(): kept, = lax.optimization_barrier((keep_part.reshape(shape),))]
    unnamed x12 -> x8, local copies, waits for them, and re-layouts: 6.25 us -> 6.84 us
  transfers between devices with their start and end apart: 7 -> 6, of which waited for: 4 -> 4; matrix products, arithmetic and copies ran while one was open for 17% -> 19% of each run, Pallas kernels for 0% -> 0%
where the time goes in v7:
time: 269 us; the launch traced here: 266 us
  waiting for transfers between devices  163 us (61%)
  matrix products  48.2 us (18%)
  local copies, waits for them, and re-layouts  28.3 us (11%)
  between operations  13.5 us (5%)
  other arithmetic  9.55 us (4%)
  starting transfers between devices  3.47 us (1%)
    ppermute x1, waiting for transfers between devices, shards(): other_b = lax.ppermute(masked_b, 'ylo', [(0, 1), (1, 0)])  62.5 us
    reduce_scatter x1, waiting for transfers between devices, shards(): summed = lax.psum_scatter(summed, 'z', scatter_dimension=0, tiled=True)  56.6 us
    dot_general x2, matrix products, product(): jnp.einsum('tka,kn->tan', flat_a, src[lo:hi], precision=lax.Precision.HIG...  48.2 us
    all_gather x1, waiting for transfers between devices, shards(): lax.all_gather(local_a[:, c * step:(c + 1) * step], 'x', axis=0, tiled=True)  36.4 us
    dynamic_slice x2, local copies, waits for them, and re-layouts, shards(): send_b = lax.dynamic_index_in_dim(both_b, 1 - core, 0, keepdims=False)  8.86 us
    another operation x3, local copies, waits for them, and re-layouts, shards(): jnp.stack([masked_b.reshape(depth, width), other_b.reshape(depth, width)])  8.18 us
    ppermute x1, waiting for transfers between devices, shards(): lax.ppermute(first, AXES, perms[0]) + lax.ppermute(second, AXES, perms[1])  7.14 us
    unnamed x8, local copies, waits for them, and re-layouts  6.84 us
  transfers between devices with their start and end apart: 6, of which 4 were waited for; matrix products, arithmetic and copies ran while one was open for 19% of the time, Pallas kernels for 0%

profile of v7, /device:TPU:24, one launch (start us, length us, event | category | flops | bytes accessed | tf_op | source)
XLA Modules:
  0.0 265.6 jit_solution(7521389292545258698)
XLA Ops:
  6.5 2.4 copy.18
  9.0 2.0 multiply_bitcast_fusion
  11.0 0.6 copy-done.1
  11.6 0.1 copy.19
  11.7 2.6 broadcast_multiply_fusion
  14.3 0.8 collective-permute-start
  15.1 2.9 %stack_reshape.6 = f32[1,1536,512]{2,1,0:T(8,128)} reshape(f32[12,128,4,128]{3,2,1,0:T(4,128)S(1)} %broadcast_multiply_fusion) | data formatting | bytes 6291456 | tf_op jit(solution)/shard_map/stack;reshape | solution.py:38
  18.0 3.8 %constant_dynamic-update-slice_fusion.1 = f32[2,1536,512]{2,1,0:T(8,128)} fusion(f32[1,1536,512]{2,1,0:T(8,128)} %stack_reshape.6), kind=kLoop, calls=%fused_computation.4 | loop fusion | bytes 6291456
  21.9 62.5 %collective-permute-done = f32[12,128,4,128]{3,2,1,0:T(4,128)} collective-permute-done((f32[12,128,4,128]{3,2,1,0:T(4,128)S(1)}, f32[12,128,4,128]{3,2,1,0:T(4,128)}, u32[]{:S(2)}, u32[]{:S(2)}) %collective-permute-start) | collective-permute-done | bytes 3145760 | tf_op jit(solution)/shard_map/ppermute | solution.py:34
  84.3 3.3 %stack_reshape.7 = f32[1,1536,512]{2,1,0:T(8,128)S(1)} reshape(f32[12,128,4,128]{3,2,1,0:T(4,128)} %collective-permute-done) | data formatting | bytes 6291456 | tf_op jit(solution)/shard_map/stack;reshape | solution.py:38
  87.7 2.0 constant_dynamic-update-slice_fusion
  89.6 5.3 %constant_dynamic-slice_fusion.2 = (f32[1,1536,512]{2,1,0:T(8,128)}, f32[1,1536,512]{2,1,0:T(8,128)S(1)}) fusion(f32[2,1536,512]{2,1,0:T(8,128)} %constant_dynamic-update-slice_fusion, s32[]{:T(128)S(6)} %select_n.15, s32[]{:T(128)S(6)} %select_n.14), kind=kLoop, calls=%fused_computation.7 | loop fusion | bytes 12582920 | tf_op jit(solution)/shard_map/jit(dynamic_index_in_dim)/dynamic_slice | solution.py:41
  94.9 3.6 %copy.22 = f32[1,1536,512]{1,2,0:T(8,128)} copy(f32[1,1536,512]{2,1,0:T(8,128)} %get-tuple-element.5) | data formatting | bytes 6291456 | tf_op jit(solution)/shard_map/jit(dynamic_index_in_dim)/dynamic_slice | solution.py:41
  98.5 36.4 %all-gather.2.cloned.1.call-done = f32[16,12,128,128]{3,2,1,0:T(8,128)} async-done(((f32[4,12,128,128]{3,2,1,0:T(8,128)}), f32[16,12,128,128]{3,2,1,0:T(8,128)}) %all-gather.2.cloned.1.call-update) | async-done | bytes 12582928 | tf_op jit(solution)/shard_map/all_gather | solution.py:46
  134.9 24.3 %fusion.1 = f32[16,128,4,128]{3,1,2,0:T(8,128)} fusion(f32[16,1536,128,1]{2,1,3,0:T(8,128)} %bitcast.30, f32[4,128,1536,1]{2,1,0,3:T(8,128)} %bitcast.28), kind=kOutput, calls=%fused_computation.11 | convolution fusion | flops 9663676416 | bytes 19922944 | tf_op jit(solution)/shard_map/tka,kn->tan/dot_general | solution.py:51
  159.1 2.4 copy.20
  161.5 23.9 %fusion = f32[16,128,4,128]{3,1,2,0:T(8,128)S(1)} fusion(f32[16,1536,128,1]{2,1,3,0:T(8,128)} %bitcast.31, f32[4,128,1536,1]{2,1,0,3:T(8,128)} %bitcast.29), kind=kOutput, calls=%fused_computation.10 | convolution fusion | flops 9663676416 | bytes 19922944 | tf_op jit(solution)/shard_map/tka,kn->tan/dot_general | solution.py:51
  185.5 4.9 %add.26 = f32[16,128,4,128]{3,1,2,0:T(8,128)} add(f32[16,128,4,128]{3,1,2,0:T(8,128)S(1)} %fusion, f32[16,128,4,128]{3,1,2,0:T(8,128)} %collective-permute-done.1) | non-fusion elementwise | flops 1048576 | bytes 12582912 | tf_op jit(solution)/shard_map/add | solution.py:60
  190.4 56.6 %reduce-scatter.2.cloned.1.call-done = f32[2,128,4,128]{3,1,2,0:T(8,128)} async-done(((f32[16,128,4,128]{3,1,2,0:T(8,128)}), f32[2,128,4,128]{3,1,2,0:T(8,128)}) %reduce-scatter.2.cloned.1.call-update) | async-done | bytes 524304 | tf_op jit(solution)/shard_map/reduce_scatter | solution.py:61
  247.0 1.1 constant_dynamic-slice_fusion
  248.1 1.9 collective-permute-start.2
  250.0 0.7 collective-permute-start.3
  250.7 7.1 %collective-permute-done.2 = f32[1,128,4,128]{3,1,2,0:T(8,128)S(1)} collective-permute-done((f32[1,128,4,128]{3,1,2,0:T(8,128)S(1)}, f32[1,128,4,128]{3,1,2,0:T(8,128)S(1)}, u32[]{:S(2)}, u32[]{:S(2)}) %collective-permute-start.2) | collective-permute-done | bytes 262176 | tf_op jit(solution)/shard_map/ppermute | solution.py:65
  257.9 0.9 copy.24
  (16 shorter events, 0.2 us)
Async XLA Ops:
  6.5 2.4 copy-start
  6.5 128.3 %all-gather.2.cloned.1.call-start = ((), (), s32[]{:S(2)}) async-start(), calls=%async_computation.1 | async-start | bytes 15728640 | tf_op jit(solution)/shard_map/all_gather | solution.py:46
  10.9 0.7 copy-start.1
  10.9 236.1 %reduce-scatter.2.cloned.1.call-start = ((), (), s32[]{:S(2)}) async-start(), calls=%async_computation.2 | async-start | bytes 4718592 | tf_op jit(solution)/shard_map/reduce_scatter | solution.py:61
  14.3 70.0 %collective-permute-start = (f32[12,128,4,128]{3,2,1,0:T(4,128)S(1)}, f32[12,128,4,128]{3,2,1,0:T(4,128)}, u32[]{:S(2)}, u32[]{:S(2)}) collective-permute-start(f32[12,128,4,128]{3,2,1,0:T(4,128)S(1)} %broadcast_multiply_fusion), channel_id=1, source_target_pairs={{0,4},{4,0},{1,5},{5,1},{2,6},{6,2},{3,7},{7,3},{8,12},{12,8},{9,1... | collective-permute-start | bytes 9437192 | tf_op jit(solution)/shard_map/ppermute | solution.py:34
  159.1 26.3 %collective-permute-start.1 = (f32[16,128,4,128]{3,1,2,0:T(8,128)}, f32[16,128,4,128]{3,1,2,0:T(8,128)}, u32[]{:S(2)}, u32[]{:S(2)}) collective-permute-start(f32[16,128,4,128]{3,1,2,0:T(8,128)} %fusion.1), channel_id=1, source_target_pairs={{0,8},{8,0},{1,9},{9,1},{2,10},{10,2},{3,11},{11,3},{4,12},{12,4},... | collective-permute-start | bytes 12582920 | tf_op jit(solution)/shard_map/ppermute | solution.py:58
  190.4 60.3 %copy-start.2 = (s32[1,4]{1,0:T(1,128)S(1)}, s32[1,4]{1,0:T(1,128)}, u32[]{:S(2)}) copy-start(s32[1,4]{1,0:T(1,128)} %param.9) | copy-start | bytes 52
  248.1 9.8 %collective-permute-start.2 = (f32[1,128,4,128]{3,1,2,0:T(8,128)S(1)}, f32[1,128,4,128]{3,1,2,0:T(8,128)S(1)}, u32[]{:S(2)}, u32[]{:S(2)}) collective-permute-start(f32[1,128,4,128]{3,1,2,0:T(8,128)S(1)} %get-tuple-element.8), channel_id=1, source_target_pairs={{0,0},{1,1},{2,2},{3,3},{4,132},{5,133},{6,134},{7,135},{8,4},{9,5... | collective-permute-start | bytes 786440 | tf_op jit(solution)/shard_map/ppermute | solution.py:65
  250.0 7.8 %collective-permute-start.3 = (f32[1,128,4,128]{3,1,2,0:T(8,128)S(1)}, f32[1,128,4,128]{3,1,2,0:T(8,128)S(1)}, u32[]{:S(2)}, u32[]{:S(2)}) collective-permute-start(f32[1,128,4,128]{3,1,2,0:T(8,128)S(1)} %get-tuple-element.7), channel_id=1, source_target_pairs={{0,8},{1,9},{2,10},{3,11},{4,140},{5,141},{6,142},{7,143},{8,12},{... | collective-permute-start | bytes 786440 | tf_op jit(solution)/shard_map/ppermute | solution.py:65
Sparse Core Ops, SparseCore 0:
  11.1 123.7 all-gather.1
  190.5 56.4 reduce-scatter.1
